TPU v7x, 512 devices: a whole 4x8x8 slice. The times are simulated.
512 devices in a mesh: section: 8 (over y), peer: 64 (over x, z, core).
Axes of the slice: x: 4, y: 8, z: 8, core: 2. Of those that a mesh axis runs over, the one named last changes fastest.
Arguments:
- inputs: bfloat16 [8192, 2560], P('peer'), may hold values from -6 to 6
- norm_gain: bfloat16 [8, 2560], P('section'), may hold values from 0.099609375 to 1.8984375
- w_down: bfloat16 [8, 64, 192, 2560], P('section', 'peer'), may hold values from -0.125 to 0.125
- w_up: bfloat16 [8, 64, 192, 2560], P('section', 'peer'), may hold values from -0.4375 to 0.4375
- routes: int32 [7, 2, 64, 64], replicated, may hold values from 0 to 63, as said below
- bit_order: int32 [6], replicated, may hold values from 0 to 5, each once
Outputs:
- grad_shards: float32 [8, 983040], P('section', 'peer')
Inputs may be any that keep to these rules, and one draw needn't show every extreme that they name: For each boundary s and micro-batch m, the lists routes[s, m, p, :] of all replicas p hold the same 64 distinct lanes, each list in its own order. `bit_order`: each bit number appears once.
All inputs are finite; a program needn't handle non-finite values.
Results may differ from a plain program's by a relative error of at most 0.023.
Values may be sent and summed in bfloat16 or wider, within the bound.
No kernel may reach another device: no remote copies, remote signals or barrier semaphores. Data moves between devices by JAX's collectives and lax.ppermute only.
A program may use at most 128 MiB of HBM per device.

v0:
```python
from functools import partial

import jax
import jax.numpy as jnp
from jax import lax
from jax.sharding import PartitionSpec as P

gelu_scale = 0.7978845608028654
gelu_cubic = 0.044715
norm_eps = 1e-05


def swapped(value, axis, apart):
    mask = 2**apart
    pairs = [(source, source ^ mask) for source in range(lax.axis_size(axis))]
    return lax.ppermute(value, axis, pairs)


def from_behind(value, axis, steps):
    count = lax.axis_size(axis)
    initial, last = (max(0, -steps), min(count, count - steps))
    return lax.ppermute(value, axis, [(source, source + steps) for source in range(initial, last)])


def gelu_parts(hidden):
    tangent = jnp.tanh(gelu_scale * (hidden + gelu_cubic * hidden * hidden * hidden))
    gelu_value = 0.5 * hidden * (1.0 + tangent)
    gelu_slope = 0.5 * (1.0 + tangent) + 0.5 * hidden * (1.0 - tangent * tangent) * gelu_scale * (
        1.0 + 3.0 * gelu_cubic * hidden * hidden
    )
    return (gelu_value, gelu_slope)


def normalize(row_block, gain_row):
    x_float = row_block.astype(jnp.float32)
    inv_rms = lax.rsqrt(jnp.mean(x_float * x_float, axis=-1, keepdims=True) + norm_eps)
    normed = (x_float * inv_rms * gain_row.astype(jnp.float32)).astype(jnp.bfloat16)
    return (x_float, inv_rms, normed)


def contract_last(left, right):
    return lax.dot_general(
        left, right, (((1,), (1,)), ((), ())), preferred_element_type=jnp.float32
    )


def contract_first(left, right):
    return lax.dot_general(
        left, right, (((0,), (0,)), ((), ())), preferred_element_type=jnp.float32
    )


def layer_forward(row_block, gain_row, down_proj, up_proj):
    x_float, inv_rms, normed = normalize(row_block, gain_row)
    hidden = contract_last(normed, down_proj)
    gelu_value, gelu_slope = gelu_parts(hidden)
    active = gelu_value.astype(jnp.bfloat16)
    return (x_float + jnp.dot(active, up_proj, preferred_element_type=jnp.float32)).astype(
        jnp.bfloat16
    )


def layer_backward(row_block, upstream, gain_row, down_proj, up_proj):
    x_float, inv_rms, normed = normalize(row_block, gain_row)
    hidden = contract_last(normed, down_proj)
    gelu_value, gelu_slope = gelu_parts(hidden)
    active = gelu_value.astype(jnp.bfloat16)
    grad_up = contract_first(active, upstream)
    grad_active = contract_last(upstream, up_proj)
    grad_hidden = (grad_active * gelu_slope).astype(jnp.bfloat16)
    grad_down = contract_first(grad_hidden, normed)
    grad_normed = jnp.dot(
        grad_hidden, down_proj, preferred_element_type=jnp.float32
    ) * gain_row.astype(jnp.float32)
    inner_term = jnp.mean(grad_normed * x_float, axis=-1, keepdims=True)
    grad_rows = (
        upstream.astype(jnp.float32)
        + inv_rms * (grad_normed - x_float * inv_rms * inv_rms * inner_term)
    ).astype(jnp.bfloat16)
    return (grad_rows, grad_down, grad_up)


def pack_lanes(row_block, own_lanes, peer_now, peer_count, lane_depth):
    feature_count = row_block.shape[1]
    lane_rows = (
        jnp.zeros((lane_depth * peer_count, feature_count), row_block.dtype)
        .at[own_lanes]
        .set(row_block)
    )
    lane_rows = lane_rows.reshape(lane_depth, peer_count, feature_count)
    return jnp.take(
        lane_rows, (jnp.arange(peer_count, dtype=jnp.int32) - peer_now) % peer_count, axis=1
    )


def lane_positions(all_lanes, peer_now, peer_count):
    used_lanes = jnp.sort(all_lanes[0])
    return used_lanes // peer_count * peer_count + (peer_now - used_lanes % peer_count) % peer_count


def unpack_arrivals(received, positions):
    return received.reshape(-1, received.shape[2])[positions]


def pack_returns(gradients, positions, peer_count, lane_depth):
    feature_count = gradients.shape[1]
    lane_rows = (
        jnp.zeros((lane_depth * peer_count, feature_count), gradients.dtype)
        .at[positions]
        .set(gradients)
    )
    return lane_rows.reshape(lane_depth, peer_count, feature_count)


def unpack_returns(came_back, own_lanes, peer_now, peer_count):
    unrolled = jnp.take(
        came_back, (jnp.arange(peer_count, dtype=jnp.int32) + peer_now) % peer_count, axis=1
    )
    return unrolled.reshape(-1, came_back.shape[2])[own_lanes]


def trade_half(values, bit):
    return swapped(values, "peer", bit)


def local(inputs, norm_gain, w_down, w_up, routes, bit_order):
    sections = lax.axis_size("section")
    peer_count = lax.axis_size("peer")
    section_now = lax.axis_index("section")
    peer_now = lax.axis_index("peer")
    down_proj = w_down[0, 0]
    up_proj = w_up[0, 0]
    gain_row = norm_gain[0]
    micro_count = routes.shape[1]
    batch_rows = routes.shape[3]
    feature_count = inputs.shape[1]
    lane_depth = (batch_rows + peer_count - 1) // peer_count
    pieces = inputs.reshape(micro_count, batch_rows, feature_count)
    step_count = micro_count + sections - 1
    micro_ids = jnp.arange(micro_count, dtype=jnp.int32)

    def routing(boundary, micro):
        table = routes[jnp.clip(boundary, 0, sections - 2), jnp.clip(micro, 0, micro_count - 1)]
        return (table[peer_now], lane_positions(table, peer_now, peer_count))

    saved_rows = jnp.zeros((micro_count, batch_rows, feature_count), jnp.bfloat16)
    final_rows = jnp.zeros((micro_count, batch_rows, feature_count), jnp.bfloat16)
    arrived = jnp.zeros((batch_rows, feature_count), jnp.bfloat16)
    for t in range(step_count):
        micro = t - section_now
        buffer = jnp.where(section_now == 0, pieces[min(t, micro_count - 1)], arrived)
        outputs = layer_forward(buffer, gain_row, down_proj, up_proj)
        slot_mask = (micro_ids == micro)[:, None, None]
        saved_rows = jnp.where(slot_mask, buffer[None], saved_rows)
        final_rows = jnp.where(slot_mask, outputs[None], final_rows)
        if t < step_count - 1:
            own_lanes, positions = routing(section_now, micro)
            outgoing = pack_lanes(outputs, own_lanes, peer_now, peer_count, lane_depth)
            received = lax.all_to_all(outgoing, "peer", split_axis=1, concat_axis=1, tiled=True)
            routed = unpack_arrivals(received, positions)
            arrived = from_behind(routed, "section", 1)
    sum_down = jnp.zeros(down_proj.shape, jnp.float32)
    sum_up = jnp.zeros(up_proj.shape, jnp.float32)
    arrived_grad = jnp.zeros((batch_rows, feature_count), jnp.bfloat16)
    for t in range(step_count):
        micro = t - (sections - 1 - section_now)
        picked = jnp.clip(micro, 0, micro_count - 1)
        row_block = saved_rows[picked]
        upstream = jnp.where(section_now == sections - 1, final_rows[picked], arrived_grad)
        grad_rows, grad_down, grad_up = layer_backward(
            row_block, upstream, gain_row, down_proj, up_proj
        )
        valid = (micro >= 0) & (micro < micro_count)
        sum_down = sum_down + jnp.where(valid, grad_down, 0.0)
        sum_up = sum_up + jnp.where(valid, grad_up, 0.0)
        if t < step_count - 1:
            moved_down = from_behind(grad_rows, "section", -1)
            own_lanes, positions = routing(section_now, t - sections + 2 + section_now)
            outgoing = pack_returns(moved_down, positions, peer_count, lane_depth)
            came_back = lax.all_to_all(outgoing, "peer", split_axis=1, concat_axis=1, tiled=True)
            arrived_grad = unpack_returns(came_back, own_lanes, peer_now, peer_count)
    gradient = jnp.concatenate([sum_down.reshape(-1), sum_up.reshape(-1)])
    bits_count = peer_count.bit_length() - 1
    branches = [partial(trade_half, bit=b) for b in range(bits_count)]
    current = gradient
    for k in range(bits_count):
        chosen = bit_order[k]
        own_bit = jnp.right_shift(peer_now, chosen) & 1
        half_len = current.shape[0] // 2
        lower_half = current[:half_len]
        upper_half = current[half_len:]
        outgoing = jnp.where(own_bit == 0, upper_half, lower_half)
        kept_half = jnp.where(own_bit == 0, lower_half, upper_half)
        current = kept_half + lax.switch(chosen, branches, outgoing)
    return (current * (1.0 / peer_count)).reshape(1, -1)


def solution(mesh):
    placed = (
        P("peer", None),
        P("section", None),
        P("section", "peer", None, None),
        P("section", "peer", None, None),
        P(),
        P(),
    )
    return jax.shard_map(
        local, mesh=mesh, in_specs=placed, out_specs=P("section", "peer"), check_vma=False
    )
```

profile of v0, /device:TPU:6, one launch (start us, length us, event | category | flops | bytes accessed | tf_op | source)
XLA Modules:
  0.0 1066.1 jit_solution(14897538116942589081)
XLA Ops:
  11.9 14.0 %all-to-all-start = ((bf16[64,2,1280]{2,1,0:T(2,128)(2,1)}), bf16[64,2,1280]{2,1,0:T(2,128)(2,1)S(1)}, u32[]{:S(2)}, u32[]{:S(2)}) async-start(bf16[64,2,1280]{2,1,0:T(2,128)(2,1)} %reshape.1648), calls=%async_computation | async-start | bytes 655360 | tf_op jit(solution)/shard_map/all_to_all | solution.py:159
  29.1 9.7 all-to-all-done
  72.2 10.7 all-to-all-done.1
  118.5 10.8 %all-to-all-done.2 = bf16[64,2,1280]{2,1,0:T(2,128)(2,1)S(1)} async-done(((bf16[64,2,1280]{2,1,0:T(2,128)(2,1)}), bf16[64,2,1280]{2,1,0:T(2,128)(2,1)S(1)}, u32[]{:S(2)}, u32[]{:S(2)}) %all-to-all-start.2) | async-done | bytes 327712 | tf_op jit(solution)/shard_map/all_to_all | solution.py:159
  165.2 10.7 all-to-all-done.3
  271.0 10.3 all-to-all-start.5
  281.4 12.8 %all-to-all-done.5 = bf16[64,2,1280]{2,1,0:T(2,128)(2,1)S(1)} async-done(((bf16[64,2,1280]{2,1,0:T(2,128)(2,1)}), bf16[64,2,1280]{2,1,0:T(2,128)(2,1)S(1)}, u32[]{:S(2)}, u32[]{:S(2)}) %all-to-all-start.5) | async-done | bytes 327712 | tf_op jit(solution)/shard_map/all_to_all | solution.py:159
  331.2 10.5 all-to-all-done.6
  379.1 11.1 %all-to-all-done.7 = bf16[64,2,1280]{2,1,0:T(2,128)(2,1)S(1)} async-done(((bf16[64,2,1280]{2,1,0:T(2,128)(2,1)}), bf16[64,2,1280]{2,1,0:T(2,128)(2,1)S(1)}, u32[]{:S(2)}, u32[]{:S(2)}) %all-to-all-start.7) | async-done | bytes 327712 | tf_op jit(solution)/shard_map/all_to_all | solution.py:159
  415.8 11.5 %collective-permute-done.44 = bf16[64,2560]{1,0:T(8,128)(2,1)} collective-permute-done((bf16[64,2560]{1,0:T(8,128)(2,1)S(1)}, bf16[64,2560]{1,0:T(8,128)(2,1)}, u32[]{:S(2)}, u32[]{:S(2)}) %collective-permute-start.44) | collective-permute-done | bytes 327712 | tf_op jit(solution)/shard_map/ppermute | solution.py:22
  445.1 12.1 %all-to-all-done.8 = bf16[64,2,1280]{2,1,0:T(2,128)(2,1)} async-done(((bf16[64,2,1280]{2,1,0:T(2,128)(2,1)}), bf16[64,2,1280]{2,1,0:T(2,128)(2,1)}, u32[]{:S(2)}, u32[]{:S(2)}) %all-to-all-start.8) | async-done | bytes 327712 | tf_op jit(solution)/shard_map/all_to_all | solution.py:180
  474.4 11.2 %collective-permute-done.45 = bf16[64,2560]{1,0:T(8,128)(2,1)} collective-permute-done((bf16[64,2560]{1,0:T(8,128)(2,1)S(1)}, bf16[64,2560]{1,0:T(8,128)(2,1)}, u32[]{:S(2)}, u32[]{:S(2)}) %collective-permute-start.45) | collective-permute-done | bytes 327712 | tf_op jit(solution)/shard_map/ppermute | solution.py:22
  503.7 11.8 %all-to-all-done.9 = bf16[64,2,1280]{2,1,0:T(2,128)(2,1)} async-done(((bf16[64,2,1280]{2,1,0:T(2,128)(2,1)}), bf16[64,2,1280]{2,1,0:T(2,128)(2,1)}, u32[]{:S(2)}, u32[]{:S(2)}) %all-to-all-start.9) | async-done | bytes 327712 | tf_op jit(solution)/shard_map/all_to_all | solution.py:180
  532.0 11.9 %collective-permute-done.46 = bf16[64,2560]{1,0:T(8,128)(2,1)} collective-permute-done((bf16[64,2560]{1,0:T(8,128)(2,1)S(1)}, bf16[64,2560]{1,0:T(8,128)(2,1)}, u32[]{:S(2)}, u32[]{:S(2)}) %collective-permute-start.46) | collective-permute-done | bytes 327712 | tf_op jit(solution)/shard_map/ppermute | solution.py:22
  563.4 10.7 %all-to-all-done.10 = bf16[64,2,1280]{2,1,0:T(2,128)(2,1)} async-done(((bf16[64,2,1280]{2,1,0:T(2,128)(2,1)}), bf16[64,2,1280]{2,1,0:T(2,128)(2,1)}, u32[]{:S(2)}, u32[]{:S(2)}) %all-to-all-start.10) | async-done | bytes 327712 | tf_op jit(solution)/shard_map/all_to_all | solution.py:180
  591.7 11.3 %collective-permute-done.47 = bf16[64,2560]{1,0:T(8,128)(2,1)} collective-permute-done((bf16[64,2560]{1,0:T(8,128)(2,1)S(1)}, bf16[64,2560]{1,0:T(8,128)(2,1)}, u32[]{:S(2)}, u32[]{:S(2)}) %collective-permute-start.47) | collective-permute-done | bytes 327712 | tf_op jit(solution)/shard_map/ppermute | solution.py:22
  623.0 9.9 all-to-all-done.11
  891.2 93.6 %conditional.6 = (f32[491520]{0:T(1024)}) conditional(s32[]{:T(128)} %clamp.146, f32[491520]{0:T(1024)} %select_n.1073, f32[491520]{0:T(1024)} %select_n.1073, f32[491520]{0:T(1024)} %select_n.1073, f32[491520]{0:T(1024)} %select_n.1073, f32[491520]{0:T(1024)} %select_n.1073, f32[491520]{0:T(1024)} %select_n.1073), branch_computations={%region_58.60_spmd, %region_59.61_spmd, %region_60.62_spmd, %regio... | conditional | bytes 7864368 | solution.py:194
  894.3 90.5 %collective-permute-done.3 = f32[491520]{0:T(1024)} collective-permute-done((f32[491520]{0:T(1024)}, f32[491520]{0:T(1024)}, u32[]{:S(2)}, u32[]{:S(2)}) %collective-permute-start.3) | collective-permute-done | bytes 1966112 | tf_op jit(solution)/shard_map/cond/branch_3_fun/ppermute | solution.py:16
  987.2 25.7 %conditional.7 = (f32[245760]{0:T(1024)}) conditional(s32[]{:T(128)} %clamp.147, f32[245760]{0:T(1024)S(1)} %slice_select_fusion, f32[245760]{0:T(1024)S(1)} %slice_select_fusion, f32[245760]{0:T(1024)S(1)} %slice_select_fusion, f32[245760]{0:T(1024)S(1)} %slice_select_fusion, ...), branch_computations={%region_64.66_spmd, %region_65.67_spmd, %region_66.68_spmd, %regio... | conditional | bytes 3932208 | solution.py:194
  989.9 23.0 %collective-permute-done.10 = f32[245760]{0:T(1024)} collective-permute-done((f32[245760]{0:T(1024)S(1)}, f32[245760]{0:T(1024)}, u32[]{:S(2)}, u32[]{:S(2)}) %collective-permute-start.10) | collective-permute-done | bytes 983072 | tf_op jit(solution)/shard_map/cond/branch_4_fun/ppermute | solution.py:16
  1015.3 24.8 %conditional.8 = (f32[122880]{0:T(1024)}) conditional(s32[]{:T(128)} %clamp.148, f32[122880]{0:T(1024)S(1)} %slice_select_fusion.1, f32[122880]{0:T(1024)S(1)} %slice_select_fusion.1, f32[122880]{0:T(1024)S(1)} %slice_select_fusion.1, f32[122880]{0:T(1024)S(1)} %slice_select_fusion.1, ...), branch_computations={%region_70.72_spmd, %region_71.73_spmd, %region_72.74_spmd, %regio... | conditional | bytes 1966128 | solution.py:194
  1017.2 22.8 %collective-permute-done.14 = f32[122880]{0:T(1024)} collective-permute-done((f32[122880]{0:T(1024)S(1)}, f32[122880]{0:T(1024)}, u32[]{:S(2)}, u32[]{:S(2)}) %collective-permute-start.14) | collective-permute-done | bytes 491552 | tf_op jit(solution)/shard_map/cond/branch_2_fun/ppermute | solution.py:16
  1041.5 9.9 conditional.9
  (566 shorter events, 740.0 us)
Async XLA Ops:
  11.9 26.9 %all-to-all-start = ((bf16[64,2,1280]{2,1,0:T(2,128)(2,1)}), bf16[64,2,1280]{2,1,0:T(2,128)(2,1)S(1)}, u32[]{:S(2)}, u32[]{:S(2)}) async-start(bf16[64,2,1280]{2,1,0:T(2,128)(2,1)} %reshape.1648), calls=%async_computation | async-start | bytes 655360 | tf_op jit(solution)/shard_map/all_to_all | solution.py:159
  63.5 19.3 %all-to-all-start.1 = ((bf16[64,2,1280]{2,1,0:T(2,128)(2,1)}), bf16[64,2,1280]{2,1,0:T(2,128)(2,1)S(1)}, u32[]{:S(2)}, u32[]{:S(2)}) async-start(bf16[64,2,1280]{2,1,0:T(2,128)(2,1)} %reshape.1650), calls=%async_computation.1 | async-start | bytes 655360 | tf_op jit(solution)/shard_map/all_to_all | solution.py:159
  110.1 19.1 %all-to-all-start.2 = ((bf16[64,2,1280]{2,1,0:T(2,128)(2,1)}), bf16[64,2,1280]{2,1,0:T(2,128)(2,1)S(1)}, u32[]{:S(2)}, u32[]{:S(2)}) async-start(bf16[64,2,1280]{2,1,0:T(2,128)(2,1)} %reshape.1652), calls=%async_computation.2 | async-start | bytes 655360 | tf_op jit(solution)/shard_map/all_to_all | solution.py:159
  156.6 19.3 %all-to-all-start.3 = ((bf16[64,2,1280]{2,1,0:T(2,128)(2,1)}), bf16[64,2,1280]{2,1,0:T(2,128)(2,1)S(1)}, u32[]{:S(2)}, u32[]{:S(2)}) async-start(bf16[64,2,1280]{2,1,0:T(2,128)(2,1)} %reshape.1654), calls=%async_computation.3 | async-start | bytes 655360 | tf_op jit(solution)/shard_map/all_to_all | solution.py:159
  203.2 39.2 %all-to-all-start.4 = ((bf16[64,2,1280]{2,1,0:T(2,128)(2,1)}), bf16[64,2,1280]{2,1,0:T(2,128)(2,1)S(1)}, u32[]{:S(2)}, u32[]{:S(2)}) async-start(bf16[64,2,1280]{2,1,0:T(2,128)(2,1)} %reshape.1656), calls=%async_computation.4 | async-start | bytes 655360 | tf_op jit(solution)/shard_map/all_to_all | solution.py:159
  271.0 23.2 %all-to-all-start.5 = ((bf16[64,2,1280]{2,1,0:T(2,128)(2,1)}), bf16[64,2,1280]{2,1,0:T(2,128)(2,1)S(1)}, u32[]{:S(2)}, u32[]{:S(2)}) async-start(bf16[64,2,1280]{2,1,0:T(2,128)(2,1)} %reshape.1658), calls=%async_computation.5 | async-start | bytes 655360 | tf_op jit(solution)/shard_map/all_to_all | solution.py:159
  322.6 19.1 %all-to-all-start.6 = ((bf16[64,2,1280]{2,1,0:T(2,128)(2,1)}), bf16[64,2,1280]{2,1,0:T(2,128)(2,1)S(1)}, u32[]{:S(2)}, u32[]{:S(2)}) async-start(bf16[64,2,1280]{2,1,0:T(2,128)(2,1)} %reshape.1660), calls=%async_computation.6 | async-start | bytes 655360 | tf_op jit(solution)/shard_map/all_to_all | solution.py:159
  371.0 19.1 %all-to-all-start.7 = ((bf16[64,2,1280]{2,1,0:T(2,128)(2,1)}), bf16[64,2,1280]{2,1,0:T(2,128)(2,1)S(1)}, u32[]{:S(2)}, u32[]{:S(2)}) async-start(bf16[64,2,1280]{2,1,0:T(2,128)(2,1)} %reshape.1662), calls=%async_computation.7 | async-start | bytes 655360 | tf_op jit(solution)/shard_map/all_to_all | solution.py:159
  393.8 13.2 %collective-permute-start.43 = (bf16[64,2560]{1,0:T(8,128)(2,1)}, bf16[64,2560]{1,0:T(8,128)(2,1)S(1)}, u32[]{:S(2)}, u32[]{:S(2)}) collective-permute-start(bf16[64,2560]{1,0:T(8,128)(2,1)} %gather_fusion.7), channel_id=1, source_target_pairs={{0,64},{64,128},{128,192},{192,256},{256,320},{320,384},{384,448},... | collective-permute-start | bytes 983048 | tf_op jit(solution)/shard_map/ppermute | solution.py:22
  437.9 19.3 %all-to-all-start.8 = ((bf16[64,2,1280]{2,1,0:T(2,128)(2,1)}), bf16[64,2,1280]{2,1,0:T(2,128)(2,1)}, u32[]{:S(2)}, u32[]{:S(2)}) async-start(bf16[64,2,1280]{2,1,0:T(2,128)(2,1)} %reshape.1664), calls=%async_computation.8 | async-start | bytes 655360 | tf_op jit(solution)/shard_map/all_to_all | solution.py:180
  471.9 13.7 %collective-permute-start.45 = (bf16[64,2560]{1,0:T(8,128)(2,1)S(1)}, bf16[64,2560]{1,0:T(8,128)(2,1)}, u32[]{:S(2)}, u32[]{:S(2)}) collective-permute-start(bf16[64,2560]{1,0:T(8,128)(2,1)S(1)} %fusion.180), channel_id=1, source_target_pairs={{64,0},{128,64},{192,128},{256,192},{320,256},{384,320},{448,384},... | collective-permute-start | bytes 983048 | tf_op jit(solution)/shard_map/ppermute | solution.py:22
  496.2 19.2 %all-to-all-start.9 = ((bf16[64,2,1280]{2,1,0:T(2,128)(2,1)}), bf16[64,2,1280]{2,1,0:T(2,128)(2,1)}, u32[]{:S(2)}, u32[]{:S(2)}) async-start(bf16[64,2,1280]{2,1,0:T(2,128)(2,1)} %reshape.1666), calls=%async_computation.9 | async-start | bytes 655360 | tf_op jit(solution)/shard_map/all_to_all | solution.py:180
  530.2 13.7 %collective-permute-start.46 = (bf16[64,2560]{1,0:T(8,128)(2,1)S(1)}, bf16[64,2560]{1,0:T(8,128)(2,1)}, u32[]{:S(2)}, u32[]{:S(2)}) collective-permute-start(bf16[64,2560]{1,0:T(8,128)(2,1)S(1)} %fusion.174), channel_id=1, source_target_pairs={{64,0},{128,64},{192,128},{256,192},{320,256},{384,320},{448,384},... | collective-permute-start | bytes 983048 | tf_op jit(solution)/shard_map/ppermute | solution.py:22
  554.9 19.2 %all-to-all-start.10 = ((bf16[64,2,1280]{2,1,0:T(2,128)(2,1)}), bf16[64,2,1280]{2,1,0:T(2,128)(2,1)}, u32[]{:S(2)}, u32[]{:S(2)}) async-start(bf16[64,2,1280]{2,1,0:T(2,128)(2,1)} %reshape.1668), calls=%async_computation.10 | async-start | bytes 655360 | tf_op jit(solution)/shard_map/all_to_all | solution.py:180
  589.3 13.7 %collective-permute-start.47 = (bf16[64,2560]{1,0:T(8,128)(2,1)S(1)}, bf16[64,2560]{1,0:T(8,128)(2,1)}, u32[]{:S(2)}, u32[]{:S(2)}) collective-permute-start(bf16[64,2560]{1,0:T(8,128)(2,1)S(1)} %fusion.168), channel_id=1, source_target_pairs={{64,0},{128,64},{192,128},{256,192},{320,256},{384,320},{448,384},... | collective-permute-start | bytes 983048 | tf_op jit(solution)/shard_map/ppermute | solution.py:22
  613.5 19.4 %all-to-all-start.11 = ((bf16[64,2,1280]{2,1,0:T(2,128)(2,1)}), bf16[64,2,1280]{2,1,0:T(2,128)(2,1)}, u32[]{:S(2)}, u32[]{:S(2)}) async-start(bf16[64,2,1280]{2,1,0:T(2,128)(2,1)} %reshape.1670), calls=%async_computation.11 | async-start | bytes 655360 | tf_op jit(solution)/shard_map/all_to_all | solution.py:180
  671.6 19.2 %all-to-all-start.12 = ((bf16[64,2,1280]{2,1,0:T(2,128)(2,1)}), bf16[64,2,1280]{2,1,0:T(2,128)(2,1)}, u32[]{:S(2)}, u32[]{:S(2)}) async-start(bf16[64,2,1280]{2,1,0:T(2,128)(2,1)} %reshape.1672), calls=%async_computation.12 | async-start | bytes 655360 | tf_op jit(solution)/shard_map/all_to_all | solution.py:180
  729.8 19.2 %all-to-all-start.13 = ((bf16[64,2,1280]{2,1,0:T(2,128)(2,1)}), bf16[64,2,1280]{2,1,0:T(2,128)(2,1)}, u32[]{:S(2)}, u32[]{:S(2)}) async-start(bf16[64,2,1280]{2,1,0:T(2,128)(2,1)} %reshape.1674), calls=%async_computation.13 | async-start | bytes 655360 | tf_op jit(solution)/shard_map/all_to_all | solution.py:180
  788.2 19.2 %all-to-all-start.14 = ((bf16[64,2,1280]{2,1,0:T(2,128)(2,1)}), bf16[64,2,1280]{2,1,0:T(2,128)(2,1)}, u32[]{:S(2)}, u32[]{:S(2)}) async-start(bf16[64,2,1280]{2,1,0:T(2,128)(2,1)} %reshape.1676), calls=%async_computation.14 | async-start | bytes 655360 | tf_op jit(solution)/shard_map/all_to_all | solution.py:180
  822.4 13.2 %collective-permute-start.51 = (bf16[64,2560]{1,0:T(8,128)(2,1)S(1)}, bf16[64,2560]{1,0:T(8,128)(2,1)}, u32[]{:S(2)}, u32[]{:S(2)}) collective-permute-start(bf16[64,2560]{1,0:T(8,128)(2,1)S(1)} %fusion.144), channel_id=1, source_target_pairs={{64,0},{128,64},{192,128},{256,192},{320,256},{384,320},{448,384},... | collective-permute-start | bytes 983048 | tf_op jit(solution)/shard_map/ppermute | solution.py:22
  846.2 19.2 %all-to-all-start.15 = ((bf16[64,2,1280]{2,1,0:T(2,128)(2,1)}), bf16[64,2,1280]{2,1,0:T(2,128)(2,1)}, u32[]{:S(2)}, u32[]{:S(2)}) async-start(bf16[64,2,1280]{2,1,0:T(2,128)(2,1)} %reshape.1678), calls=%async_computation.15 | async-start | bytes 655360 | tf_op jit(solution)/shard_map/all_to_all | solution.py:180
  891.2 93.6 %collective-permute-start.3 = (f32[491520]{0:T(1024)}, f32[491520]{0:T(1024)}, u32[]{:S(2)}, u32[]{:S(2)}) collective-permute-start(f32[491520]{0:T(1024)} %param.5), channel_id=1, source_target_pairs={{0,8},{1,9},{2,10},{3,11},{4,12},{5,13},{6,14},{7,15},{8,0},{9,1},... | collective-permute-start | bytes 5898248 | tf_op jit(solution)/shard_map/cond/branch_3_fun/ppermute | solution.py:16
  987.3 25.6 %collective-permute-start.10 = (f32[245760]{0:T(1024)S(1)}, f32[245760]{0:T(1024)}, u32[]{:S(2)}, u32[]{:S(2)}) collective-permute-start(f32[245760]{0:T(1024)S(1)} %param.12), channel_id=1, source_target_pairs={{0,16},{1,17},{2,18},{3,19},{4,20},{5,21},{6,22},{7,23},{8,24},{9,... | collective-permute-start | bytes 2949128 | tf_op jit(solution)/shard_map/cond/branch_4_fun/ppermute | solution.py:16
  1015.3 24.7 %collective-permute-start.14 = (f32[122880]{0:T(1024)S(1)}, f32[122880]{0:T(1024)}, u32[]{:S(2)}, u32[]{:S(2)}) collective-permute-start(f32[122880]{0:T(1024)S(1)} %param.16), channel_id=1, source_target_pairs={{0,4},{1,5},{2,6},{3,7},{4,0},{5,1},{6,2},{7,3},{8,12},{9,13},{10,... | collective-permute-start | bytes 1474568 | tf_op jit(solution)/shard_map/cond/branch_2_fun/ppermute | solution.py:16
  (102 other events, 854.2 us)
where the time goes:
time: 1090 us; the launch traced here: 1070 us
  waiting for transfers between devices  439 us (40%)
  local copies, waits for them, and re-layouts  216 us (20%)
  starting transfers between devices  179 us (16%)
  other arithmetic  142 us (13%)
  matrix products  79.8 us (7%)
    all_to_all x16, waiting for transfers between devices, local(): lax.all_to_all(outgoing, 'peer', split_axis=1, concat_axis=1, tiled=True)  151 us
    ppermute x6, waiting for transfers between devices, swapped(): return lax.ppermute(value, axis, pairs)  151 us
    ppermute x16, waiting for transfers between devices, from_behind(): lax.ppermute(value, axis, [(source, source + steps) for source in range(i...  137 us
    all_to_all x16, starting transfers between devices, local(): lax.all_to_all(outgoing, 'peer', split_axis=1, concat_axis=1, tiled=True)  114 us
    unnamed x225, local copies, waits for them, and re-layouts  81 us
    unnamed x16, other arithmetic  61 us
    ppermute x16, starting transfers between devices, from_behind(): lax.ppermute(value, axis, [(source, source + steps) for source in range(i...  49.9 us
    dot_general x18, matrix products, contract_first(): lax.dot_general(left, right, (((0,), (0,)), ((), ())), preferred_element_...  43.6 us
  transfers between devices with their start and end apart: 38, of which 37 were waited for; matrix products, arithmetic and copies ran while one was open for 8% of the time, Pallas kernels for 0%

commit v1 on v0

v1 whole, which is shorter than its diff:
```python
import jax
import jax.numpy as jnp
from jax import lax
from jax.sharding import PartitionSpec as P

gelu_scale = 0.7978845608028654
gelu_cubic = 0.044715
norm_eps = 1e-05


def gelu_parts(hidden):
    tangent = jnp.tanh(gelu_scale * (hidden + gelu_cubic * hidden * hidden * hidden))
    gelu_value = 0.5 * hidden * (1.0 + tangent)
    gelu_slope = 0.5 * (1.0 + tangent) + 0.5 * hidden * (1.0 - tangent * tangent) * gelu_scale * (
        1.0 + 3.0 * gelu_cubic * hidden * hidden
    )
    return (gelu_value, gelu_slope)


def normalize(row_block, gain_row):
    x_float = row_block.astype(jnp.float32)
    inv_rms = lax.rsqrt(jnp.mean(x_float * x_float, axis=-1, keepdims=True) + norm_eps)
    normed = (x_float * inv_rms * gain_row.astype(jnp.float32)).astype(jnp.bfloat16)
    return (x_float, inv_rms, normed)


def contract_last(left, right):
    return lax.dot_general(
        left, right, (((1,), (1,)), ((), ())), preferred_element_type=jnp.float32
    )


def contract_first(left, right):
    return lax.dot_general(
        left, right, (((0,), (0,)), ((), ())), preferred_element_type=jnp.float32
    )


def permute_rows(onehot, rows, spec):
    return jnp.einsum(spec, onehot, rows, preferred_element_type=jnp.float32).astype(rows.dtype)


def local(inputs, norm_gain, w_down, w_up, routes, bit_order):
    sections = lax.axis_size("section")
    peer_count = lax.axis_size("peer")
    section_now = lax.axis_index("section")
    peer_now = lax.axis_index("peer")
    down_proj = w_down[0, 0]
    up_proj = w_up[0, 0]
    gain_row = norm_gain[0]
    gain_float = gain_row.astype(jnp.float32)
    micro_count = routes.shape[1]
    batch_rows = routes.shape[3]
    feature_count = inputs.shape[1]
    row_count = micro_count * batch_rows

    slots = jnp.arange(batch_rows, dtype=jnp.int32)
    own_lanes = routes[:, :, peer_now, :]
    arrived_rows = (peer_now - slots) % batch_rows
    slot_lanes = jnp.concatenate(
        [own_lanes[:1], jnp.take(own_lanes[1:], arrived_rows, axis=2)], axis=0
    )
    destinations = (peer_now + slot_lanes) % peer_count
    send_onehot = (
        destinations[:, :, None, :] == jnp.arange(peer_count, dtype=jnp.int32)[None, None, :, None]
    ).astype(jnp.bfloat16)

    x = inputs.reshape(micro_count, batch_rows, feature_count)
    keep_x = jnp.zeros((row_count, feature_count), jnp.bfloat16)
    keep_inv = jnp.zeros((row_count, 1), jnp.float32)
    keep_normed = jnp.zeros((row_count, feature_count), jnp.bfloat16)
    keep_active = jnp.zeros((row_count, down_proj.shape[0]), jnp.bfloat16)
    keep_slope = jnp.zeros((row_count, down_proj.shape[0]), jnp.float32)
    upstream = None
    for k in range(sections):
        flat = x.reshape(row_count, feature_count)
        x_float, inv_rms, normed = normalize(flat, gain_row)
        hidden = contract_last(normed, down_proj)
        gelu_value, gelu_slope = gelu_parts(hidden)
        active = gelu_value.astype(jnp.bfloat16)
        outputs = (x_float + jnp.dot(active, up_proj, preferred_element_type=jnp.float32)).astype(
            jnp.bfloat16
        )
        mine = section_now == k
        keep_x = jnp.where(mine, flat, keep_x)
        keep_inv = jnp.where(mine, inv_rms, keep_inv)
        keep_normed = jnp.where(mine, normed, keep_normed)
        keep_active = jnp.where(mine, active, keep_active)
        keep_slope = jnp.where(mine, gelu_slope, keep_slope)
        if k < sections - 1:
            packed = permute_rows(
                send_onehot[k], outputs.reshape(micro_count, batch_rows, feature_count), "mdq,mqf->mdf"
            )
            received = lax.all_to_all(packed, "peer", 1, 1, tiled=True)
            x = lax.ppermute(received, "section", [(k, k + 1)])
        else:
            upstream = outputs

    x_float = keep_x.astype(jnp.float32)
    keep_upstream = jnp.zeros((row_count, feature_count), jnp.bfloat16)
    keep_grad_hidden = jnp.zeros((row_count, down_proj.shape[0]), jnp.bfloat16)
    for k in reversed(range(sections)):
        grad_active = contract_last(upstream, up_proj)
        grad_hidden = (grad_active * keep_slope).astype(jnp.bfloat16)
        grad_normed = jnp.dot(grad_hidden, down_proj, preferred_element_type=jnp.float32) * gain_float
        inner_term = jnp.mean(grad_normed * x_float, axis=-1, keepdims=True)
        grad_rows = (
            upstream.astype(jnp.float32)
            + keep_inv * (grad_normed - x_float * keep_inv * keep_inv * inner_term)
        ).astype(jnp.bfloat16)
        mine = section_now == k
        keep_upstream = jnp.where(mine, upstream, keep_upstream)
        keep_grad_hidden = jnp.where(mine, grad_hidden, keep_grad_hidden)
        if k > 0:
            sent = lax.all_to_all(
                grad_rows.reshape(micro_count, batch_rows, feature_count), "peer", 1, 1, tiled=True
            )
            moved = lax.ppermute(sent, "section", [(k, k - 1)])
            upstream = permute_rows(send_onehot[k - 1], moved, "mdq,mdf->mqf").reshape(
                row_count, feature_count
            )

    sum_down = contract_first(keep_grad_hidden, keep_normed)
    sum_up = contract_first(keep_active, keep_upstream)
    gradient = jnp.concatenate([sum_down.reshape(-1), sum_up.reshape(-1)]).reshape(peer_count, -1)
    bits_count = peer_count.bit_length() - 1
    peers = jnp.arange(peer_count, dtype=jnp.int32)
    bit_table = jnp.right_shift(peers[:, None], bit_order[None, :]) & 1
    weights = jnp.left_shift(jnp.int32(1), bits_count - 1 - jnp.arange(bits_count, dtype=jnp.int32))
    shard_of = jnp.sum(bit_table * weights[None, :], axis=1).astype(jnp.int32)
    ordered = jnp.take(gradient, shard_of, axis=0)
    shard = lax.psum_scatter(ordered, "peer", scatter_dimension=0, tiled=True)
    return (shard * (1.0 / peer_count)).reshape(1, -1)


def solution(mesh):
    placed = (
        P("peer", None),
        P("section", None),
        P("section", "peer", None, None),
        P("section", "peer", None, None),
        P(),
        P(),
    )
    return jax.shard_map(
        local, mesh=mesh, in_specs=placed, out_specs=P("section", "peer"), check_vma=False
    )
```

time: 1090 us -> 931 us (0.85); the launches traced: 1070 us -> 920 us
  blocking collectives: 0 us -> 372 us
  local copies, waits for them, and re-layouts: 216 us -> 31.5 us
  starting transfers between devices: 179 us -> 15 us
  other arithmetic: 142 us -> 22.7 us
  matrix products: 79.8 us -> 38.2 us
  waiting for transfers between devices: 439 us -> 425 us
    all_to_all x0 -> x14, blocking collectives: none -> 372 us  [the longest x7 189 us: local(): received = lax.all_to_all(packed, 'peer', 1, 1, tiled=True)]
    unnamed x0 -> x2, waiting for transfers between devices: none -> 197 us
    all_to_all x16 -> x0, waiting for transfers between devices: 151 us -> none  [local(): lax.all_to_all(outgoing, 'peer', split_axis=1, concat_axis=1, tiled=True)]
    all_to_all x16 -> x0, starting transfers between devices: 114 us -> none  [local(): lax.all_to_all(outgoing, 'peer', split_axis=1, concat_axis=1, tiled=True)]
    unnamed x225 -> x100, local copies, waits for them, and re-layouts: 81 us -> 3.43 us
    gather x32 -> x2, local copies, waits for them, and re-layouts: 69.7 us -> 7.97 us  [the longest x1 7.31 us: local(): ordered = jnp.take(gradient, shard_of, axis=0)]
    unnamed x16 -> x0, other arithmetic: 61 us -> none
    ppermute x22 -> x14, waiting for transfers between devices: 288 us -> 228 us  [the longest x7 214 us: local(): moved = lax.ppermute(sent, 'section', [(k, k - 1)])]
  transfers between devices with their start and end apart: 38 -> 15, of which waited for: 37 -> 3; matrix products, arithmetic and copies ran while one was open for 8% -> 0% of each run, Pallas kernels for 0% -> 0%
where the time goes in v1:
time: 931 us; the launch traced here: 920 us
  waiting for transfers between devices  425 us (46%)
  blocking collectives  372 us (40%)
  matrix products  38.2 us (4%)
  local copies, waits for them, and re-layouts  31.5 us (3%)
  other arithmetic  22.7 us (2%)
  starting transfers between devices  15 us (2%)
  between operations  14.9 us (2%)
    ppermute x7, waiting for transfers between devices, local(): moved = lax.ppermute(sent, 'section', [(k, k - 1)])  214 us
    unnamed x2, waiting for transfers between devices  197 us
    all_to_all x7, blocking collectives, local(): received = lax.all_to_all(packed, 'peer', 1, 1, tiled=True)  189 us
    all_to_all x7, blocking collectives, local(): lax.all_to_all(grad_rows.reshape(micro_count, batch_rows, feature_count),...  183 us
  transfers between devices with their start and end apart: 15, of which 3 were waited for; matrix products, arithmetic and copies ran while one was open for 0% of the time, Pallas kernels for 0%

profile of v1, /device:TPU:6, one launch (start us, length us, event | category | flops | bytes accessed | tf_op | source)
XLA Modules:
  0.0 919.5 jit_solution(5778684831407338140)
XLA Ops:
  15.6 33.1 %all_to_all.70 = bf16[2,64,2560]{2,0,1:T(2,128)(2,1)S(1)} all-to-all(bf16[2,64,2560]{2,0,1:T(2,128)(2,1)S(1)} %copy.111), channel_id=1, replica_groups=mesh['section'=8,'peer'=64] {'peer'}, dimensions={1} | all-to-all | bytes 1310720 | tf_op jit(solution)/shard_map/all_to_all | solution.py:94
  48.8 3.6 collective-permute-start
  52.4 14.9 %collective-permute-done = bf16[2,64,2560]{2,1,0:T(8,128)(2,1)S(1)} collective-permute-done((bf16[2,64,2560]{2,1,0:T(8,128)(2,1)S(1)}, bf16[2,64,2560]{2,1,0:T(8,128)(2,1)S(1)}, u32[]{:S(2)}, u32[]{:S(2)}) %collective-permute-start) | collective-permute-done | bytes 655392 | tf_op jit(solution)/shard_map/ppermute | solution.py:95
  69.6 25.2 %all_to_all.71 = bf16[2,64,2560]{2,0,1:T(2,128)(2,1)S(1)} all-to-all(bf16[2,64,2560]{2,0,1:T(2,128)(2,1)S(1)} %copy.113), channel_id=1, replica_groups=mesh['section'=8,'peer'=64] {'peer'}, dimensions={1} | all-to-all | bytes 1310720 | tf_op jit(solution)/shard_map/all_to_all | solution.py:94
  97.9 26.2 %all_to_all.72 = bf16[2,64,2560]{2,0,1:T(2,128)(2,1)S(1)} all-to-all(bf16[2,64,2560]{2,0,1:T(2,128)(2,1)S(1)} %copy.115), channel_id=1, replica_groups=mesh['section'=8,'peer'=64] {'peer'}, dimensions={1} | all-to-all | bytes 1310720 | tf_op jit(solution)/shard_map/all_to_all | solution.py:94
  127.2 26.1 %all_to_all.73 = bf16[2,64,2560]{2,0,1:T(2,128)(2,1)S(1)} all-to-all(bf16[2,64,2560]{2,0,1:T(2,128)(2,1)S(1)} %copy.117), channel_id=1, replica_groups=mesh['section'=8,'peer'=64] {'peer'}, dimensions={1} | all-to-all | bytes 1310720 | tf_op jit(solution)/shard_map/all_to_all | solution.py:94
  156.5 26.1 %all_to_all.74 = bf16[2,64,2560]{2,0,1:T(2,128)(2,1)S(1)} all-to-all(bf16[2,64,2560]{2,0,1:T(2,128)(2,1)S(1)} %copy.119), channel_id=1, replica_groups=mesh['section'=8,'peer'=64] {'peer'}, dimensions={1} | all-to-all | bytes 1310720 | tf_op jit(solution)/shard_map/all_to_all | solution.py:94
  185.7 26.1 %all_to_all.75 = bf16[2,64,2560]{2,0,1:T(2,128)(2,1)S(1)} all-to-all(bf16[2,64,2560]{2,0,1:T(2,128)(2,1)S(1)} %copy.121), channel_id=1, replica_groups=mesh['section'=8,'peer'=64] {'peer'}, dimensions={1} | all-to-all | bytes 1310720 | tf_op jit(solution)/shard_map/all_to_all | solution.py:94
  215.0 26.1 %all_to_all.76 = bf16[2,64,2560]{2,0,1:T(2,128)(2,1)S(1)} all-to-all(bf16[2,64,2560]{2,0,1:T(2,128)(2,1)S(1)} %copy.123), channel_id=1, replica_groups=mesh['section'=8,'peer'=64] {'peer'}, dimensions={1} | all-to-all | bytes 1310720 | tf_op jit(solution)/shard_map/all_to_all | solution.py:94
  255.8 26.2 %all_to_all.77 = bf16[2,64,2560]{2,0,1:T(2,128)(2,1)S(1)} all-to-all(bf16[2,64,2560]{2,0,1:T(2,128)(2,1)S(1)} %copy.125), channel_id=1, replica_groups=mesh['section'=8,'peer'=64] {'peer'}, dimensions={1} | all-to-all | bytes 1310720 | tf_op jit(solution)/shard_map/all_to_all | solution.py:115
  286.0 26.1 %all_to_all.78 = bf16[2,64,2560]{2,0,1:T(2,128)(2,1)S(1)} all-to-all(bf16[2,64,2560]{2,0,1:T(2,128)(2,1)S(1)} %copy.128), channel_id=1, replica_groups=mesh['section'=8,'peer'=64] {'peer'}, dimensions={1} | all-to-all | bytes 1310720 | tf_op jit(solution)/shard_map/all_to_all | solution.py:115
  316.2 26.2 %all_to_all.79 = bf16[2,64,2560]{2,0,1:T(2,128)(2,1)S(1)} all-to-all(bf16[2,64,2560]{2,0,1:T(2,128)(2,1)S(1)} %copy.131), channel_id=1, replica_groups=mesh['section'=8,'peer'=64] {'peer'}, dimensions={1} | all-to-all | bytes 1310720 | tf_op jit(solution)/shard_map/all_to_all | solution.py:115
  346.9 26.1 %all_to_all.80 = bf16[2,64,2560]{2,0,1:T(2,128)(2,1)S(1)} all-to-all(bf16[2,64,2560]{2,0,1:T(2,128)(2,1)S(1)} %copy.134), channel_id=1, replica_groups=mesh['section'=8,'peer'=64] {'peer'}, dimensions={1} | all-to-all | bytes 1310720 | tf_op jit(solution)/shard_map/all_to_all | solution.py:115
  377.1 26.2 %all_to_all.81 = bf16[2,64,2560]{2,0,1:T(2,128)(2,1)S(1)} all-to-all(bf16[2,64,2560]{2,0,1:T(2,128)(2,1)S(1)} %copy.137), channel_id=1, replica_groups=mesh['section'=8,'peer'=64] {'peer'}, dimensions={1} | all-to-all | bytes 1310720 | tf_op jit(solution)/shard_map/all_to_all | solution.py:115
  407.3 26.2 %all_to_all.82 = bf16[2,64,2560]{2,0,1:T(2,128)(2,1)S(1)} all-to-all(bf16[2,64,2560]{2,0,1:T(2,128)(2,1)S(1)} %copy.140), channel_id=1, replica_groups=mesh['section'=8,'peer'=64] {'peer'}, dimensions={1} | all-to-all | bytes 1310720 | tf_op jit(solution)/shard_map/all_to_all | solution.py:115
  437.6 26.2 %all_to_all.83 = bf16[2,64,2560]{2,0,1:T(2,128)(2,1)S(1)} all-to-all(bf16[2,64,2560]{2,0,1:T(2,128)(2,1)S(1)} %copy.143), channel_id=1, replica_groups=mesh['section'=8,'peer'=64] {'peer'}, dimensions={1} | all-to-all | bytes 1310720 | tf_op jit(solution)/shard_map/all_to_all | solution.py:115
  465.3 213.5 %collective-permute-done.13 = bf16[2,64,2560]{2,1,0:T(8,128)(2,1)S(1)} collective-permute-done((bf16[2,64,2560]{2,1,0:T(8,128)(2,1)S(1)}, bf16[2,64,2560]{2,1,0:T(8,128)(2,1)S(1)}, u32[]{:S(2)}, u32[]{:S(2)}) %collective-permute-start.13) | collective-permute-done | bytes 655392 | tf_op jit(solution)/shard_map/ppermute | solution.py:118
  680.9 5.5 fusion.98
  686.5 3.4 fusion.153
  693.2 3.3 concatenate.20
  696.5 4.3 pad_maximum_fusion
  700.8 7.3 gather_fusion.1
  708.1 4.3 broadcast_select_fusion
  713.7 196.6 %all-reduce.3.cloned.1.call-done = f32[64,15360]{1,0:T(8,128)} async-done(((f32[64,15360]{1,0:T(8,128)}), f32[64,15360]{1,0:T(8,128)}) %all-reduce.3.cloned.1.call-update) | async-done | bytes 3932176
  (260 shorter events, 75.7 us)
Async XLA Ops:
  6.5 903.7 %all-reduce.3.cloned.1.call-start = ((), (), s32[]{:S(2)}) async-start(), calls=%async_computation.14 | async-start | bytes 7864320
  10.0 203.9 %copy-start.20 = (pred[7,2,64,64]{3,2,1,0:T(32,128)(4,1)}, pred[7,2,64,64]{3,2,1,0:T(32,128)(4,1)S(1)}, u32[]{:S(2)}) copy-start(pred[7,2,64,64]{3,2,1,0:T(32,128)(4,1)S(1)} %iota_compare_fusion) | copy-start | bytes 172036
  48.8 19.0 %copy-start.1 = (bf16[1,1,192,2560]{3,2,1,0:T(8,128)(2,1)S(1)}, bf16[1,1,192,2560]{3,2,1,0:T(8,128)(2,1)}, u32[]{:S(2)}) copy-start(bf16[1,1,192,2560]{3,2,1,0:T(8,128)(2,1)} %param.8) | copy-start | bytes 2949124
  48.8 18.5 %collective-permute-start = (bf16[2,64,2560]{2,1,0:T(8,128)(2,1)S(1)}, bf16[2,64,2560]{2,1,0:T(8,128)(2,1)S(1)}, u32[]{:S(2)}, u32[]{:S(2)}) collective-permute-start(bf16[2,64,2560]{2,1,0:T(8,128)(2,1)S(1)} %copy.112), channel_id=1, source_target_pairs={{0,64},{1,65},{2,66},{3,67},{4,68},{5,69},{6,70},{7,71},{8,72},{9,... | collective-permute-start | bytes 1966088 | tf_op jit(solution)/shard_map/ppermute | solution.py:95
  94.9 0.7 collective-permute-start.1
  124.2 0.7 collective-permute-start.2
  153.4 0.7 collective-permute-start.3
  182.7 0.7 collective-permute-start.4
  211.9 0.7 collective-permute-start.5
  242.0 2.3 collective-permute-start.6
  244.2 10.4 %copy-start.39 = (f32[128]{0:T(128)}, f32[128]{0:T(128)S(1)}, u32[]{:S(2)}) copy-start(f32[128]{0:T(128)S(1)} %rsqrt.127) | copy-start | bytes 1540
  282.1 0.7 collective-permute-start.7
  312.2 0.7 collective-permute-start.8
  342.4 1.1 collective-permute-start.9
  373.1 0.7 collective-permute-start.10
  403.3 0.7 collective-permute-start.11
  433.6 0.7 collective-permute-start.12
  463.8 217.1 %copy-start.4 = (bf16[2,64,2560]{2,1,0:T(8,128)(2,1)S(1)}, bf16[2,64,2560]{2,1,0:T(8,128)(2,1)}, u32[]{:S(2)}) copy-start(bf16[2,64,2560]{2,1,0:T(8,128)(2,1)} %copy-done.2) | copy-start | bytes 1966084
  463.8 217.1 %copy-start.40 = (f32[128]{0:T(128)S(1)}, f32[128]{0:T(128)}, u32[]{:S(2)}) copy-start(f32[128]{0:T(128)} %copy-done.39) | copy-start | bytes 1540
  463.8 217.1 %copy-start.42 = (f32[128]{0:T(128)S(1)}, f32[128]{0:T(128)}, u32[]{:S(2)}) copy-start(f32[128]{0:T(128)} %copy-done.41) | copy-start | bytes 1540
  463.8 217.1 %copy-start.44 = (f32[128]{0:T(128)S(1)}, f32[128]{0:T(128)}, u32[]{:S(2)}) copy-start(f32[128]{0:T(128)} %copy-done.43) | copy-start | bytes 1540
  463.8 217.1 %copy-start.46 = (f32[128]{0:T(128)S(1)}, f32[128]{0:T(128)}, u32[]{:S(2)}) copy-start(f32[128]{0:T(128)} %copy-done.45) | copy-start | bytes 1540
  463.8 217.1 %copy-start.48 = (f32[128]{0:T(128)S(1)}, f32[128]{0:T(128)}, u32[]{:S(2)}) copy-start(f32[128]{0:T(128)} %copy-done.47) | copy-start | bytes 1540
  463.9 215.0 %collective-permute-start.13 = (bf16[2,64,2560]{2,1,0:T(8,128)(2,1)S(1)}, bf16[2,64,2560]{2,1,0:T(8,128)(2,1)S(1)}, u32[]{:S(2)}, u32[]{:S(2)}) collective-permute-start(bf16[2,64,2560]{2,1,0:T(8,128)(2,1)S(1)} %copy.144), channel_id=1, source_target_pairs={{64,0},{65,1},{66,2},{67,3},{68,4},{69,5},{70,6},{71,7},{72,8},{73... | collective-permute-start | bytes 1966088 | tf_op jit(solution)/shard_map/ppermute | solution.py:118
  (40 other events, 99.8 us)
Sparse Core Ops, SparseCore 0:
  712.6 197.6 all-reduce.2

commit v2 on v1

--- a/solution.py
+++ b/solution.py
@@ -120,17 +120,34 @@
                 row_count, feature_count
             )
 
-    sum_down = contract_first(keep_grad_hidden, keep_normed)
-    sum_up = contract_first(keep_active, keep_upstream)
-    gradient = jnp.concatenate([sum_down.reshape(-1), sum_up.reshape(-1)]).reshape(peer_count, -1)
     bits_count = peer_count.bit_length() - 1
     peers = jnp.arange(peer_count, dtype=jnp.int32)
-    bit_table = jnp.right_shift(peers[:, None], bit_order[None, :]) & 1
+    halving_bits = [0, 1, 4, 2, 5, 3][:bits_count]
+    position_peer = jnp.zeros((peer_count,), jnp.int32)
+    for t, b in enumerate(halving_bits):
+        position_peer = position_peer + (((peers >> (bits_count - 1 - t)) & 1) << b)
+    bit_table = jnp.right_shift(position_peer[:, None], bit_order[None, :]) & 1
     weights = jnp.left_shift(jnp.int32(1), bits_count - 1 - jnp.arange(bits_count, dtype=jnp.int32))
-    shard_of = jnp.sum(bit_table * weights[None, :], axis=1).astype(jnp.int32)
-    ordered = jnp.take(gradient, shard_of, axis=0)
-    shard = lax.psum_scatter(ordered, "peer", scatter_dimension=0, tiled=True)
-    return (shard * (1.0 / peer_count)).reshape(1, -1)
+    source_chunk = jnp.sum(bit_table * weights[None, :], axis=1).astype(jnp.int32)
+    units = down_proj.shape[0]
+    chunk_rows = 2 * units // peer_count
+    column_source = (
+        source_chunk[:, None] * chunk_rows + jnp.arange(chunk_rows, dtype=jnp.int32)[None, :]
+    ).reshape(-1)
+    left = jnp.zeros((2 * row_count, 2 * units), jnp.bfloat16)
+    left = left.at[:row_count, :units].set(keep_grad_hidden).at[row_count:, units:].set(keep_active)
+    left = jnp.take(left, column_source, axis=1)
+    right = jnp.concatenate([keep_normed, keep_upstream], axis=0)
+    current = contract_first(left, right).reshape(-1)
+    for b in halving_bits:
+        own_bit = (peer_now >> b) & 1
+        half_len = current.shape[0] // 2
+        outgoing = lax.dynamic_slice(current, ((1 - own_bit) * half_len,), (half_len,))
+        kept = lax.dynamic_slice(current, (own_bit * half_len,), (half_len,))
+        mask = 2**b
+        pairs = [(source, source ^ mask) for source in range(peer_count)]
+        current = kept + lax.ppermute(outgoing, "peer", pairs)
+    return (current * (1.0 / peer_count)).reshape(1, -1)
 
 
 def solution(mesh):

time: 931 us -> 786 us (0.84)
  waiting for transfers between devices: 425 us -> 303 us
  blocking collectives: 372 us -> 346 us
  starting transfers between devices: 15 us -> 37.9 us
  between operations: 14.9 us -> 1.85 us
    unnamed x2 -> x0, waiting for transfers between devices: 197 us -> none
    ppermute x0 -> x6, waiting for transfers between devices: none -> 63.1 us  [local(): current = kept + lax.ppermute(outgoing, 'peer', pairs)]
    all_to_all x7 -> x6, blocking collectives: 183 us -> 157 us  [local(): lax.all_to_all(grad_rows.reshape(micro_count, batch_rows, feature_count),...]
    all_to_all x0 -> x1, waiting for transfers between devices: none -> 16.6 us  [local(): lax.all_to_all(grad_rows.reshape(micro_count, batch_rows, feature_count),...]
    ppermute x0 -> x6, starting transfers between devices: none -> 15.9 us  [local(): current = kept + lax.ppermute(outgoing, 'peer', pairs)]
  transfers between devices with their start and end apart: 15 -> 21, of which waited for: 3 -> 9; matrix products, arithmetic and copies ran while one was open for 0% -> 1% of each run, Pallas kernels for 0% -> 0%
where the time goes in v2:
time: 786 us; the launch traced here: 776 us
  blocking collectives  346 us (44%)
  waiting for transfers between devices  303 us (39%)
  starting transfers between devices  37.9 us (5%)
  local copies, waits for them, and re-layouts  32.5 us (4%)
  matrix products  31.1 us (4%)
  other arithmetic  23.2 us (3%)
    ppermute x7, waiting for transfers between devices, local(): moved = lax.ppermute(sent, 'section', [(k, k - 1)])  208 us
    all_to_all x7, blocking collectives, local(): received = lax.all_to_all(packed, 'peer', 1, 1, tiled=True)  189 us
    all_to_all x6, blocking collectives, local(): lax.all_to_all(grad_rows.reshape(micro_count, batch_rows, feature_count),...  157 us
    ppermute x6, waiting for transfers between devices, local(): current = kept + lax.ppermute(outgoing, 'peer', pairs)  63.1 us
    all_to_all x1, waiting for transfers between devices, local(): lax.all_to_all(grad_rows.reshape(micro_count, batch_rows, feature_count),...  16.6 us
    ppermute x6, starting transfers between devices, local(): current = kept + lax.ppermute(outgoing, 'peer', pairs)  15.9 us
  transfers between devices with their start and end apart: 21, of which 9 were waited for; matrix products, arithmetic and copies ran while one was open for 1% of the time, Pallas kernels for 0%

profile of v2, /device:TPU:6, one launch (start us, length us, event | category | flops | bytes accessed | tf_op | source)
XLA Modules:
  0.0 775.6 jit_solution(666508604313789376)
XLA Ops:
  8.5 33.1 %all_to_all.70 = bf16[2,64,2560]{2,0,1:T(2,128)(2,1)S(1)} all-to-all(bf16[2,64,2560]{2,0,1:T(2,128)(2,1)S(1)} %copy.111), channel_id=1, replica_groups=mesh['section'=8,'peer'=64] {'peer'}, dimensions={1} | all-to-all | bytes 1310720 | tf_op jit(solution)/shard_map/all_to_all | solution.py:94
  45.3 14.9 %collective-permute-done = bf16[2,64,2560]{2,1,0:T(8,128)(2,1)S(1)} collective-permute-done((bf16[2,64,2560]{2,1,0:T(8,128)(2,1)S(1)}, bf16[2,64,2560]{2,1,0:T(8,128)(2,1)S(1)}, u32[]{:S(2)}, u32[]{:S(2)}) %collective-permute-start) | collective-permute-done | bytes 655392 | tf_op jit(solution)/shard_map/ppermute | solution.py:95
  62.4 25.2 %all_to_all.71 = bf16[2,64,2560]{2,0,1:T(2,128)(2,1)S(1)} all-to-all(bf16[2,64,2560]{2,0,1:T(2,128)(2,1)S(1)} %copy.113), channel_id=1, replica_groups=mesh['section'=8,'peer'=64] {'peer'}, dimensions={1} | all-to-all | bytes 1310720 | tf_op jit(solution)/shard_map/all_to_all | solution.py:94
  90.8 26.2 %all_to_all.72 = bf16[2,64,2560]{2,0,1:T(2,128)(2,1)S(1)} all-to-all(bf16[2,64,2560]{2,0,1:T(2,128)(2,1)S(1)} %copy.115), channel_id=1, replica_groups=mesh['section'=8,'peer'=64] {'peer'}, dimensions={1} | all-to-all | bytes 1310720 | tf_op jit(solution)/shard_map/all_to_all | solution.py:94
  120.0 26.1 %all_to_all.73 = bf16[2,64,2560]{2,0,1:T(2,128)(2,1)S(1)} all-to-all(bf16[2,64,2560]{2,0,1:T(2,128)(2,1)S(1)} %copy.117), channel_id=1, replica_groups=mesh['section'=8,'peer'=64] {'peer'}, dimensions={1} | all-to-all | bytes 1310720 | tf_op jit(solution)/shard_map/all_to_all | solution.py:94
  149.3 26.1 %all_to_all.74 = bf16[2,64,2560]{2,0,1:T(2,128)(2,1)S(1)} all-to-all(bf16[2,64,2560]{2,0,1:T(2,128)(2,1)S(1)} %copy.119), channel_id=1, replica_groups=mesh['section'=8,'peer'=64] {'peer'}, dimensions={1} | all-to-all | bytes 1310720 | tf_op jit(solution)/shard_map/all_to_all | solution.py:94
  178.5 26.1 %all_to_all.75 = bf16[2,64,2560]{2,0,1:T(2,128)(2,1)S(1)} all-to-all(bf16[2,64,2560]{2,0,1:T(2,128)(2,1)S(1)} %copy.121), channel_id=1, replica_groups=mesh['section'=8,'peer'=64] {'peer'}, dimensions={1} | all-to-all | bytes 1310720 | tf_op jit(solution)/shard_map/all_to_all | solution.py:94
  207.8 26.1 %all_to_all.76 = bf16[2,64,2560]{2,0,1:T(2,128)(2,1)S(1)} all-to-all(bf16[2,64,2560]{2,0,1:T(2,128)(2,1)S(1)} %copy.123), channel_id=1, replica_groups=mesh['section'=8,'peer'=64] {'peer'}, dimensions={1} | all-to-all | bytes 1310720 | tf_op jit(solution)/shard_map/all_to_all | solution.py:94
  249.3 26.2 %all_to_all.77 = bf16[2,64,2560]{2,0,1:T(2,128)(2,1)S(1)} all-to-all(bf16[2,64,2560]{2,0,1:T(2,128)(2,1)S(1)} %copy.125), channel_id=1, replica_groups=mesh['section'=8,'peer'=64] {'peer'}, dimensions={1} | all-to-all | bytes 1310720 | tf_op jit(solution)/shard_map/all_to_all | solution.py:115
  279.4 26.2 %all_to_all.78 = bf16[2,64,2560]{2,0,1:T(2,128)(2,1)S(1)} all-to-all(bf16[2,64,2560]{2,0,1:T(2,128)(2,1)S(1)} %copy.128), channel_id=1, replica_groups=mesh['section'=8,'peer'=64] {'peer'}, dimensions={1} | all-to-all | bytes 1310720 | tf_op jit(solution)/shard_map/all_to_all | solution.py:115
  309.6 26.1 %all_to_all.79 = bf16[2,64,2560]{2,0,1:T(2,128)(2,1)S(1)} all-to-all(bf16[2,64,2560]{2,0,1:T(2,128)(2,1)S(1)} %copy.131), channel_id=1, replica_groups=mesh['section'=8,'peer'=64] {'peer'}, dimensions={1} | all-to-all | bytes 1310720 | tf_op jit(solution)/shard_map/all_to_all | solution.py:115
  340.3 26.2 %all_to_all.80 = bf16[2,64,2560]{2,0,1:T(2,128)(2,1)S(1)} all-to-all(bf16[2,64,2560]{2,0,1:T(2,128)(2,1)S(1)} %copy.134), channel_id=1, replica_groups=mesh['section'=8,'peer'=64] {'peer'}, dimensions={1} | all-to-all | bytes 1310720 | tf_op jit(solution)/shard_map/all_to_all | solution.py:115
  370.5 26.2 %all_to_all.81 = bf16[2,64,2560]{2,0,1:T(2,128)(2,1)S(1)} all-to-all(bf16[2,64,2560]{2,0,1:T(2,128)(2,1)S(1)} %copy.137), channel_id=1, replica_groups=mesh['section'=8,'peer'=64] {'peer'}, dimensions={1} | all-to-all | bytes 1310720 | tf_op jit(solution)/shard_map/all_to_all | solution.py:115
  400.8 26.1 %all_to_all.82 = bf16[2,64,2560]{2,0,1:T(2,128)(2,1)S(1)} all-to-all(bf16[2,64,2560]{2,0,1:T(2,128)(2,1)S(1)} %copy.140), channel_id=1, replica_groups=mesh['section'=8,'peer'=64] {'peer'}, dimensions={1} | all-to-all | bytes 1310720 | tf_op jit(solution)/shard_map/all_to_all | solution.py:115
  431.9 7.2 all-to-all-start.13
  441.8 16.6 %all-to-all-done.13 = bf16[2,64,2560]{2,0,1:T(2,128)(2,1)} async-done(((bf16[2,64,2560]{2,0,1:T(2,128)(2,1)}), bf16[2,64,2560]{2,0,1:T(2,128)(2,1)}, u32[]{:S(2)}, u32[]{:S(2)}) %all-to-all-start.13) | async-done | bytes 655392 | tf_op jit(solution)/shard_map/all_to_all | solution.py:115
  461.0 5.1 fusion.141
  466.1 208.4 %collective-permute-done.13 = bf16[2,64,2560]{2,1,0:T(8,128)(2,1)S(1)} collective-permute-done((bf16[2,64,2560]{2,1,0:T(8,128)(2,1)S(1)}, bf16[2,64,2560]{2,1,0:T(8,128)(2,1)S(1)}, u32[]{:S(2)}, u32[]{:S(2)}) %collective-permute-start.13) | collective-permute-done | bytes 655392 | tf_op jit(solution)/shard_map/ppermute | solution.py:118
  682.4 4.7 reshape.618
  700.8 23.3 %collective-permute-done.15 = f32[245760]{0:T(1024)} collective-permute-done((f32[245760]{0:T(1024)}, f32[245760]{0:T(1024)}, u32[]{:S(2)}, u32[]{:S(2)}) %collective-permute-start.15) | collective-permute-done | bytes 983072 | tf_op jit(solution)/shard_map/ppermute | solution.py:149
  729.1 11.6 %collective-permute-done.16 = f32[122880]{0:T(1024)S(1)} collective-permute-done((f32[122880]{0:T(1024)S(1)}, f32[122880]{0:T(1024)S(1)}, u32[]{:S(2)}, u32[]{:S(2)}) %collective-permute-start.16) | collective-permute-done | bytes 491552 | tf_op jit(solution)/shard_map/ppermute | solution.py:149
  744.3 11.9 %collective-permute-done.17 = f32[61440]{0:T(1024)S(1)} collective-permute-done((f32[61440]{0:T(1024)S(1)}, f32[61440]{0:T(1024)S(1)}, u32[]{:S(2)}, u32[]{:S(2)}) %collective-permute-start.17) | collective-permute-done | bytes 245792 | tf_op jit(solution)/shard_map/ppermute | solution.py:149
  759.5 5.2 collective-permute-done.18
  767.7 7.1 collective-permute-done.19
  (325 shorter events, 111.7 us)
Async XLA Ops:
  41.7 18.4 %collective-permute-start = (bf16[2,64,2560]{2,1,0:T(8,128)(2,1)S(1)}, bf16[2,64,2560]{2,1,0:T(8,128)(2,1)S(1)}, u32[]{:S(2)}, u32[]{:S(2)}) collective-permute-start(bf16[2,64,2560]{2,1,0:T(8,128)(2,1)S(1)} %copy.112), channel_id=1, source_target_pairs={{0,64},{1,65},{2,66},{3,67},{4,68},{5,69},{6,70},{7,71},{8,72},{9,... | collective-permute-start | bytes 1966088 | tf_op jit(solution)/shard_map/ppermute | solution.py:95
  87.7 0.7 collective-permute-start.1
  117.0 0.7 collective-permute-start.2
  146.2 0.7 collective-permute-start.3
  175.5 0.7 collective-permute-start.4
  204.7 0.7 collective-permute-start.5
  234.8 2.4 collective-permute-start.6
  275.5 0.7 collective-permute-start.7
  305.6 0.7 collective-permute-start.8
  335.9 1.1 collective-permute-start.9
  366.5 0.7 collective-permute-start.10
  396.7 0.7 collective-permute-start.11
  427.0 0.7 collective-permute-start.12
  431.9 26.5 %all-to-all-start.13 = ((bf16[2,64,2560]{2,0,1:T(2,128)(2,1)}), bf16[2,64,2560]{2,0,1:T(2,128)(2,1)}, u32[]{:S(2)}, u32[]{:S(2)}) async-start(bf16[2,64,2560]{2,0,1:T(2,128)(2,1)} %copy.143), calls=%async_computation.13 | async-start | bytes 1310720 | tf_op jit(solution)/shard_map/all_to_all | solution.py:115
  459.6 214.9 %collective-permute-start.13 = (bf16[2,64,2560]{2,1,0:T(8,128)(2,1)S(1)}, bf16[2,64,2560]{2,1,0:T(8,128)(2,1)S(1)}, u32[]{:S(2)}, u32[]{:S(2)}) collective-permute-start(bf16[2,64,2560]{2,1,0:T(8,128)(2,1)S(1)} %copy.144), channel_id=1, source_target_pairs={{64,0},{65,1},{66,2},{67,3},{68,4},{69,5},{70,6},{71,7},{72,8},{73... | collective-permute-start | bytes 1966088 | tf_op jit(solution)/shard_map/ppermute | solution.py:118
  460.9 214.6 %copy-start.17 = (bf16[2,64,2560]{2,1,0:T(8,128)(2,1)S(1)}, bf16[2,64,2560]{2,1,0:T(8,128)(2,1)}, u32[]{:S(2)}) copy-start(bf16[2,64,2560]{2,1,0:T(8,128)(2,1)} %copy-done.16) | copy-start | bytes 1966084
  460.9 214.6 %copy-start.19 = (bf16[2,64,2560]{2,1,0:T(8,128)(2,1)S(1)}, bf16[2,64,2560]{2,1,0:T(8,128)(2,1)}, u32[]{:S(2)}) copy-start(bf16[2,64,2560]{2,1,0:T(8,128)(2,1)} %copy-done.18) | copy-start | bytes 1966084
  460.9 214.6 %copy-start.21 = (bf16[2,64,2560]{2,1,0:T(8,128)(2,1)S(1)}, bf16[2,64,2560]{2,1,0:T(8,128)(2,1)}, u32[]{:S(2)}) copy-start(bf16[2,64,2560]{2,1,0:T(8,128)(2,1)} %copy-done.20) | copy-start | bytes 1966084
  688.8 6.0 collective-permute-start.14
  698.1 26.0 %collective-permute-start.15 = (f32[245760]{0:T(1024)}, f32[245760]{0:T(1024)}, u32[]{:S(2)}, u32[]{:S(2)}) collective-permute-start(f32[245760]{0:T(1024)} %dynamic_slice.43), channel_id=1, source_target_pairs={{0,2},{1,3},{2,0},{3,1},{4,6},{5,7},{6,4},{7,5},{8,10},{9,11},{10,... | collective-permute-start | bytes 2949128 | tf_op jit(solution)/shard_map/ppermute | solution.py:149
  726.4 14.3 %collective-permute-start.16 = (f32[122880]{0:T(1024)S(1)}, f32[122880]{0:T(1024)S(1)}, u32[]{:S(2)}, u32[]{:S(2)}) collective-permute-start(f32[122880]{0:T(1024)S(1)} %dynamic_slice.45), channel_id=1, source_target_pairs={{0,16},{1,17},{2,18},{3,19},{4,20},{5,21},{6,22},{7,23},{8,24},{9,... | collective-permute-start | bytes 1474568 | tf_op jit(solution)/shard_map/ppermute | solution.py:149
  741.9 14.3 %collective-permute-start.17 = (f32[61440]{0:T(1024)S(1)}, f32[61440]{0:T(1024)S(1)}, u32[]{:S(2)}, u32[]{:S(2)}) collective-permute-start(f32[61440]{0:T(1024)S(1)} %dynamic_slice.47), channel_id=1, source_target_pairs={{0,4},{1,5},{2,6},{3,7},{4,0},{5,1},{6,2},{7,3},{8,12},{9,13},{10,... | collective-permute-start | bytes 737288 | tf_op jit(solution)/shard_map/ppermute | solution.py:149
  756.3 8.4 %collective-permute-start.18 = (f32[30720]{0:T(1024)S(1)}, f32[30720]{0:T(1024)S(1)}, u32[]{:S(2)}, u32[]{:S(2)}) collective-permute-start(f32[30720]{0:T(1024)S(1)} %dynamic_slice.49), channel_id=1, source_target_pairs={{0,32},{1,33},{2,34},{3,35},{4,36},{5,37},{6,38},{7,39},{8,40},{9,... | collective-permute-start | bytes 368648 | tf_op jit(solution)/shard_map/ppermute | solution.py:149
  764.7 10.0 %collective-permute-start.19 = (f32[15360]{0:T(1024)S(1)}, f32[15360]{0:T(1024)S(1)}, u32[]{:S(2)}, u32[]{:S(2)}) collective-permute-start(f32[15360]{0:T(1024)S(1)} %dynamic_slice.51), channel_id=1, source_target_pairs={{0,8},{1,9},{2,10},{3,11},{4,12},{5,13},{6,14},{7,15},{8,0},{9,1},... | collective-permute-start | bytes 184328 | tf_op jit(solution)/shard_map/ppermute | solution.py:149
  (65 other events, 1194.2 us)

commit v3 on v2

--- a/solution.py
+++ b/solution.py
@@ -122,10 +122,13 @@
 
     bits_count = peer_count.bit_length() - 1
     peers = jnp.arange(peer_count, dtype=jnp.int32)
-    halving_bits = [0, 1, 4, 2, 5, 3][:bits_count]
-    position_peer = jnp.zeros((peer_count,), jnp.int32)
-    for t, b in enumerate(halving_bits):
-        position_peer = position_peer + (((peers >> (bits_count - 1 - t)) & 1) << b)
+    order_even = [1, 4, 2, 5, 3][: bits_count - 1]
+    order_odd = [4, 1, 5, 2, 3][: bits_count - 1]
+    position_core = peers >> (bits_count - 1)
+    position_peer = position_core
+    for t in range(bits_count - 1):
+        chosen = jnp.where(position_core == 0, order_even[t], order_odd[t])
+        position_peer = position_peer + (((peers >> (bits_count - 2 - t)) & 1) << chosen)
     bit_table = jnp.right_shift(position_peer[:, None], bit_order[None, :]) & 1
     weights = jnp.left_shift(jnp.int32(1), bits_count - 1 - jnp.arange(bits_count, dtype=jnp.int32))
     source_chunk = jnp.sum(bit_table * weights[None, :], axis=1).astype(jnp.int32)
@@ -138,14 +141,19 @@
     left = left.at[:row_count, :units].set(keep_grad_hidden).at[row_count:, units:].set(keep_active)
     left = jnp.take(left, column_source, axis=1)
     right = jnp.concatenate([keep_normed, keep_upstream], axis=0)
-    current = contract_first(left, right).reshape(-1)
-    for b in halving_bits:
-        own_bit = (peer_now >> b) & 1
+    current = contract_first(left, right)
+    core_now = peer_now & 1
+    stage_bits = [(0, 0)] + list(zip(order_even, order_odd))
+    for even_bit, odd_bit in stage_bits:
+        bit_now = jnp.where(core_now == 0, even_bit, odd_bit)
+        own_bit = (peer_now >> bit_now) & 1
         half_len = current.shape[0] // 2
-        outgoing = lax.dynamic_slice(current, ((1 - own_bit) * half_len,), (half_len,))
-        kept = lax.dynamic_slice(current, (own_bit * half_len,), (half_len,))
-        mask = 2**b
-        pairs = [(source, source ^ mask) for source in range(peer_count)]
+        outgoing = lax.dynamic_slice_in_dim(current, (1 - own_bit) * half_len, half_len, axis=0)
+        kept = lax.dynamic_slice_in_dim(current, own_bit * half_len, half_len, axis=0)
+        pairs = [
+            (source, source ^ (1 << (even_bit if source % 2 == 0 else odd_bit)))
+            for source in range(peer_count)
+        ]
         current = kept + lax.ppermute(outgoing, "peer", pairs)
     return (current * (1.0 / peer_count)).reshape(1, -1)
 

time: 786 us -> 766 us (0.975)
  waiting for transfers between devices: 303 us -> 287 us
    ppermute x6, waiting for transfers between devices: 63.1 us -> 47.4 us  [local(): current = kept + lax.ppermute(outgoing, 'peer', pairs)]
where the time goes in v3:
time: 766 us; the launch traced here: 756 us
  blocking collectives  346 us (45%)
  waiting for transfers between devices  287 us (37%)
  starting transfers between devices  38 us (5%)
  local copies, waits for them, and re-layouts  29.8 us (4%)
  matrix products  29.2 us (4%)
  other arithmetic  23.4 us (3%)
    ppermute x7, waiting for transfers between devices, local(): moved = lax.ppermute(sent, 'section', [(k, k - 1)])  208 us
    all_to_all x7, blocking collectives, local(): received = lax.all_to_all(packed, 'peer', 1, 1, tiled=True)  189 us
    all_to_all x6, blocking collectives, local(): lax.all_to_all(grad_rows.reshape(micro_count, batch_rows, feature_count),...  157 us
    ppermute x6, waiting for transfers between devices, local(): current = kept + lax.ppermute(outgoing, 'peer', pairs)  47.4 us
    all_to_all x1, waiting for transfers between devices, local(): lax.all_to_all(grad_rows.reshape(micro_count, batch_rows, feature_count),...  16.6 us
    ppermute x6, starting transfers between devices, local(): current = kept + lax.ppermute(outgoing, 'peer', pairs)  16 us
  transfers between devices with their start and end apart: 21, of which 9 were waited for; matrix products, arithmetic and copies ran while one was open for 1% of the time, Pallas kernels for 0%

profile of v3, /device:TPU:6, one launch (start us, length us, event | category | flops | bytes accessed | tf_op | source)
XLA Modules:
  0.0 755.7 jit_solution(6403436095145590279)
XLA Ops:
  8.3 33.1 %all_to_all.70 = bf16[2,64,2560]{2,0,1:T(2,128)(2,1)S(1)} all-to-all(bf16[2,64,2560]{2,0,1:T(2,128)(2,1)S(1)} %copy.111), channel_id=1, replica_groups=mesh['section'=8,'peer'=64] {'peer'}, dimensions={1} | all-to-all | bytes 1310720 | tf_op jit(solution)/shard_map/all_to_all | solution.py:94
  45.0 14.9 %collective-permute-done = bf16[2,64,2560]{2,1,0:T(8,128)(2,1)S(1)} collective-permute-done((bf16[2,64,2560]{2,1,0:T(8,128)(2,1)S(1)}, bf16[2,64,2560]{2,1,0:T(8,128)(2,1)S(1)}, u32[]{:S(2)}, u32[]{:S(2)}) %collective-permute-start) | collective-permute-done | bytes 655392 | tf_op jit(solution)/shard_map/ppermute | solution.py:95
  62.4 25.2 %all_to_all.71 = bf16[2,64,2560]{2,0,1:T(2,128)(2,1)S(1)} all-to-all(bf16[2,64,2560]{2,0,1:T(2,128)(2,1)S(1)} %copy.113), channel_id=1, replica_groups=mesh['section'=8,'peer'=64] {'peer'}, dimensions={1} | all-to-all | bytes 1310720 | tf_op jit(solution)/shard_map/all_to_all | solution.py:94
  90.9 26.2 %all_to_all.72 = bf16[2,64,2560]{2,0,1:T(2,128)(2,1)S(1)} all-to-all(bf16[2,64,2560]{2,0,1:T(2,128)(2,1)S(1)} %copy.115), channel_id=1, replica_groups=mesh['section'=8,'peer'=64] {'peer'}, dimensions={1} | all-to-all | bytes 1310720 | tf_op jit(solution)/shard_map/all_to_all | solution.py:94
  120.4 26.2 %all_to_all.73 = bf16[2,64,2560]{2,0,1:T(2,128)(2,1)S(1)} all-to-all(bf16[2,64,2560]{2,0,1:T(2,128)(2,1)S(1)} %copy.117), channel_id=1, replica_groups=mesh['section'=8,'peer'=64] {'peer'}, dimensions={1} | all-to-all | bytes 1310720 | tf_op jit(solution)/shard_map/all_to_all | solution.py:94
  149.9 26.2 %all_to_all.74 = bf16[2,64,2560]{2,0,1:T(2,128)(2,1)S(1)} all-to-all(bf16[2,64,2560]{2,0,1:T(2,128)(2,1)S(1)} %copy.119), channel_id=1, replica_groups=mesh['section'=8,'peer'=64] {'peer'}, dimensions={1} | all-to-all | bytes 1310720 | tf_op jit(solution)/shard_map/all_to_all | solution.py:94
  179.4 26.2 %all_to_all.75 = bf16[2,64,2560]{2,0,1:T(2,128)(2,1)S(1)} all-to-all(bf16[2,64,2560]{2,0,1:T(2,128)(2,1)S(1)} %copy.121), channel_id=1, replica_groups=mesh['section'=8,'peer'=64] {'peer'}, dimensions={1} | all-to-all | bytes 1310720 | tf_op jit(solution)/shard_map/all_to_all | solution.py:94
  208.9 26.2 %all_to_all.76 = bf16[2,64,2560]{2,0,1:T(2,128)(2,1)S(1)} all-to-all(bf16[2,64,2560]{2,0,1:T(2,128)(2,1)S(1)} %copy.123), channel_id=1, replica_groups=mesh['section'=8,'peer'=64] {'peer'}, dimensions={1} | all-to-all | bytes 1310720 | tf_op jit(solution)/shard_map/all_to_all | solution.py:94
  250.3 26.2 %all_to_all.77 = bf16[2,64,2560]{2,0,1:T(2,128)(2,1)S(1)} all-to-all(bf16[2,64,2560]{2,0,1:T(2,128)(2,1)S(1)} %copy.125), channel_id=1, replica_groups=mesh['section'=8,'peer'=64] {'peer'}, dimensions={1} | all-to-all | bytes 1310720 | tf_op jit(solution)/shard_map/all_to_all | solution.py:115
  280.5 26.2 %all_to_all.78 = bf16[2,64,2560]{2,0,1:T(2,128)(2,1)S(1)} all-to-all(bf16[2,64,2560]{2,0,1:T(2,128)(2,1)S(1)} %copy.128), channel_id=1, replica_groups=mesh['section'=8,'peer'=64] {'peer'}, dimensions={1} | all-to-all | bytes 1310720 | tf_op jit(solution)/shard_map/all_to_all | solution.py:115
  310.7 26.1 %all_to_all.79 = bf16[2,64,2560]{2,0,1:T(2,128)(2,1)S(1)} all-to-all(bf16[2,64,2560]{2,0,1:T(2,128)(2,1)S(1)} %copy.131), channel_id=1, replica_groups=mesh['section'=8,'peer'=64] {'peer'}, dimensions={1} | all-to-all | bytes 1310720 | tf_op jit(solution)/shard_map/all_to_all | solution.py:115
  341.4 26.2 %all_to_all.80 = bf16[2,64,2560]{2,0,1:T(2,128)(2,1)S(1)} all-to-all(bf16[2,64,2560]{2,0,1:T(2,128)(2,1)S(1)} %copy.134), channel_id=1, replica_groups=mesh['section'=8,'peer'=64] {'peer'}, dimensions={1} | all-to-all | bytes 1310720 | tf_op jit(solution)/shard_map/all_to_all | solution.py:115
  371.6 26.2 %all_to_all.81 = bf16[2,64,2560]{2,0,1:T(2,128)(2,1)S(1)} all-to-all(bf16[2,64,2560]{2,0,1:T(2,128)(2,1)S(1)} %copy.137), channel_id=1, replica_groups=mesh['section'=8,'peer'=64] {'peer'}, dimensions={1} | all-to-all | bytes 1310720 | tf_op jit(solution)/shard_map/all_to_all | solution.py:115
  401.9 26.1 %all_to_all.82 = bf16[2,64,2560]{2,0,1:T(2,128)(2,1)S(1)} all-to-all(bf16[2,64,2560]{2,0,1:T(2,128)(2,1)S(1)} %copy.140), channel_id=1, replica_groups=mesh['section'=8,'peer'=64] {'peer'}, dimensions={1} | all-to-all | bytes 1310720 | tf_op jit(solution)/shard_map/all_to_all | solution.py:115
  433.0 7.2 all-to-all-start.13
  442.9 16.6 %all-to-all-done.13 = bf16[2,64,2560]{2,0,1:T(2,128)(2,1)} async-done(((bf16[2,64,2560]{2,0,1:T(2,128)(2,1)}), bf16[2,64,2560]{2,0,1:T(2,128)(2,1)}, u32[]{:S(2)}, u32[]{:S(2)}) %all-to-all-start.13) | async-done | bytes 655392 | tf_op jit(solution)/shard_map/all_to_all | solution.py:115
  462.1 5.1 fusion.141
  467.2 208.3 %collective-permute-done.13 = bf16[2,64,2560]{2,1,0:T(8,128)(2,1)S(1)} collective-permute-done((bf16[2,64,2560]{2,1,0:T(8,128)(2,1)S(1)}, bf16[2,64,2560]{2,1,0:T(8,128)(2,1)S(1)}, u32[]{:S(2)}, u32[]{:S(2)}) %collective-permute-start.13) | collective-permute-done | bytes 655392 | tf_op jit(solution)/shard_map/ppermute | solution.py:118
  686.3 3.9 collective-permute-done.14
  696.3 13.6 %collective-permute-done.15 = f32[96,2560]{1,0:T(8,128)} collective-permute-done((f32[96,2560]{1,0:T(8,128)}, f32[96,2560]{1,0:T(8,128)}, u32[]{:S(2)}, u32[]{:S(2)}) %collective-permute-start.15) | collective-permute-done | bytes 983072 | tf_op jit(solution)/shard_map/ppermute | solution.py:157
  714.9 8.0 %collective-permute-done.16 = f32[48,2560]{1,0:T(8,128)S(1)} collective-permute-done((f32[48,2560]{1,0:T(8,128)S(1)}, f32[48,2560]{1,0:T(8,128)S(1)}, u32[]{:S(2)}, u32[]{:S(2)}) %collective-permute-start.16) | collective-permute-done | bytes 491552 | tf_op jit(solution)/shard_map/ppermute | solution.py:157
  726.5 9.2 %collective-permute-done.17 = f32[24,2560]{1,0:T(8,128)S(1)} collective-permute-done((f32[24,2560]{1,0:T(8,128)S(1)}, f32[24,2560]{1,0:T(8,128)S(1)}, u32[]{:S(2)}, u32[]{:S(2)}) %collective-permute-start.17) | collective-permute-done | bytes 245792 | tf_op jit(solution)/shard_map/ppermute | solution.py:157
  739.0 5.5 collective-permute-done.18
  747.6 7.2 collective-permute-done.19
  (325 shorter events, 108.1 us)
Async XLA Ops:
  41.4 18.4 %collective-permute-start = (bf16[2,64,2560]{2,1,0:T(8,128)(2,1)S(1)}, bf16[2,64,2560]{2,1,0:T(8,128)(2,1)S(1)}, u32[]{:S(2)}, u32[]{:S(2)}) collective-permute-start(bf16[2,64,2560]{2,1,0:T(8,128)(2,1)S(1)} %copy.112), channel_id=1, source_target_pairs={{0,64},{1,65},{2,66},{3,67},{4,68},{5,69},{6,70},{7,71},{8,72},{9,... | collective-permute-start | bytes 1966088 | tf_op jit(solution)/shard_map/ppermute | solution.py:95
  87.7 0.7 collective-permute-start.1
  117.2 0.7 collective-permute-start.2
  146.6 0.7 collective-permute-start.3
  176.1 0.7 collective-permute-start.4
  205.6 0.7 collective-permute-start.5
  235.9 2.4 collective-permute-start.6
  276.6 0.7 collective-permute-start.7
  306.7 0.7 collective-permute-start.8
  336.9 1.1 collective-permute-start.9
  367.6 0.7 collective-permute-start.10
  397.8 0.7 collective-permute-start.11
  428.1 0.7 collective-permute-start.12
  433.0 26.5 %all-to-all-start.13 = ((bf16[2,64,2560]{2,0,1:T(2,128)(2,1)}), bf16[2,64,2560]{2,0,1:T(2,128)(2,1)}, u32[]{:S(2)}, u32[]{:S(2)}) async-start(bf16[2,64,2560]{2,0,1:T(2,128)(2,1)} %copy.143), calls=%async_computation.13 | async-start | bytes 1310720 | tf_op jit(solution)/shard_map/all_to_all | solution.py:115
  460.7 214.8 %collective-permute-start.13 = (bf16[2,64,2560]{2,1,0:T(8,128)(2,1)S(1)}, bf16[2,64,2560]{2,1,0:T(8,128)(2,1)S(1)}, u32[]{:S(2)}, u32[]{:S(2)}) collective-permute-start(bf16[2,64,2560]{2,1,0:T(8,128)(2,1)S(1)} %copy.144), channel_id=1, source_target_pairs={{64,0},{65,1},{66,2},{67,3},{68,4},{69,5},{70,6},{71,7},{72,8},{73... | collective-permute-start | bytes 1966088 | tf_op jit(solution)/shard_map/ppermute | solution.py:118
  462.0 214.6 %copy-start.18 = (bf16[2,64,2560]{2,1,0:T(8,128)(2,1)S(1)}, bf16[2,64,2560]{2,1,0:T(8,128)(2,1)}, u32[]{:S(2)}) copy-start(bf16[2,64,2560]{2,1,0:T(8,128)(2,1)} %copy-done.17) | copy-start | bytes 1966084
  462.0 214.6 %copy-start.20 = (bf16[2,64,2560]{2,1,0:T(8,128)(2,1)S(1)}, bf16[2,64,2560]{2,1,0:T(8,128)(2,1)}, u32[]{:S(2)}) copy-start(bf16[2,64,2560]{2,1,0:T(8,128)(2,1)} %copy-done.19) | copy-start | bytes 1966084
  462.0 214.6 %copy-start.22 = (bf16[2,64,2560]{2,1,0:T(8,128)(2,1)S(1)}, bf16[2,64,2560]{2,1,0:T(8,128)(2,1)}, u32[]{:S(2)}) copy-start(bf16[2,64,2560]{2,1,0:T(8,128)(2,1)} %copy-done.21) | copy-start | bytes 1966084
  684.2 6.0 collective-permute-start.14
  693.6 16.3 %collective-permute-start.15 = (f32[96,2560]{1,0:T(8,128)}, f32[96,2560]{1,0:T(8,128)}, u32[]{:S(2)}, u32[]{:S(2)}) collective-permute-start(f32[96,2560]{1,0:T(8,128)} %constant_dynamic-slice_fusion.4), channel_id=1, source_target_pairs={{0,2},{1,17},{2,0},{3,19},{4,6},{5,21},{6,4},{7,23},{8,10},{9,25},... | collective-permute-start | bytes 2949128 | tf_op jit(solution)/shard_map/ppermute | solution.py:157
  712.2 10.7 %collective-permute-start.16 = (f32[48,2560]{1,0:T(8,128)S(1)}, f32[48,2560]{1,0:T(8,128)S(1)}, u32[]{:S(2)}, u32[]{:S(2)}) collective-permute-start(f32[48,2560]{1,0:T(8,128)S(1)} %constant_dynamic-slice_fusion.3), channel_id=1, source_target_pairs={{0,16},{1,3},{2,18},{3,1},{4,20},{5,7},{6,22},{7,5},{8,24},{9,11},... | collective-permute-start | bytes 1474568 | tf_op jit(solution)/shard_map/ppermute | solution.py:157
  724.1 11.6 %collective-permute-start.17 = (f32[24,2560]{1,0:T(8,128)S(1)}, f32[24,2560]{1,0:T(8,128)S(1)}, u32[]{:S(2)}, u32[]{:S(2)}) collective-permute-start(f32[24,2560]{1,0:T(8,128)S(1)} %constant_dynamic-slice_fusion.2), channel_id=1, source_target_pairs={{0,4},{1,33},{2,6},{3,35},{4,0},{5,37},{6,2},{7,39},{8,12},{9,41},... | collective-permute-start | bytes 737288 | tf_op jit(solution)/shard_map/ppermute | solution.py:157
  735.8 8.7 %collective-permute-start.18 = (f32[12,2560]{1,0:T(8,128)S(1)}, f32[12,2560]{1,0:T(8,128)S(1)}, u32[]{:S(2)}, u32[]{:S(2)}) collective-permute-start(f32[12,2560]{1,0:T(8,128)S(1)} %constant_dynamic-slice_fusion.1), channel_id=1, source_target_pairs={{0,32},{1,5},{2,34},{3,7},{4,36},{5,1},{6,38},{7,3},{8,40},{9,13},... | collective-permute-start | bytes 368648 | tf_op jit(solution)/shard_map/ppermute | solution.py:157
  744.5 10.2 %collective-permute-start.19 = (f32[6,2560]{1,0:T(8,128)S(1)}, f32[6,2560]{1,0:T(8,128)S(1)}, u32[]{:S(2)}, u32[]{:S(2)}) collective-permute-start(f32[6,2560]{1,0:T(8,128)S(1)} %constant_dynamic-slice_fusion), channel_id=1, source_target_pairs={{0,8},{1,9},{2,10},{3,11},{4,12},{5,13},{6,14},{7,15},{8,0},{9,1},... | collective-permute-start | bytes 184328 | tf_op jit(solution)/shard_map/ppermute | solution.py:157
  (65 other events, 1201.1 us)

commit v4 on v3

--- a/solution.py
+++ b/solution.py
@@ -154,7 +154,8 @@
             (source, source ^ (1 << (even_bit if source % 2 == 0 else odd_bit)))
             for source in range(peer_count)
         ]
-        current = kept + lax.ppermute(outgoing, "peer", pairs)
+        arrived = lax.ppermute(outgoing.astype(jnp.bfloat16), "peer", pairs)
+        current = kept + arrived.astype(jnp.float32)
     return (current * (1.0 / peer_count)).reshape(1, -1)
 
 

time: 766 us -> 752 us (0.982)
  waiting for transfers between devices: 287 us -> 274 us
    ppermute x6, waiting for transfers between devices: 47.4 us -> 34.2 us  [local(): arrived = lax.ppermute(outgoing.astype(jnp.bfloat16), 'peer', pairs)]
where the time goes in v4:
time: 752 us; the launch traced here: 742 us
  blocking collectives  346 us (46%)
  waiting for transfers between devices  274 us (36%)
  starting transfers between devices  37.8 us (5%)
  local copies, waits for them, and re-layouts  29.7 us (4%)
  matrix products  29.1 us (4%)
  other arithmetic  22.9 us (3%)
    ppermute x7, waiting for transfers between devices, local(): moved = lax.ppermute(sent, 'section', [(k, k - 1)])  209 us
    all_to_all x7, blocking collectives, local(): received = lax.all_to_all(packed, 'peer', 1, 1, tiled=True)  189 us
    all_to_all x6, blocking collectives, local(): lax.all_to_all(grad_rows.reshape(micro_count, batch_rows, feature_count),...  157 us
    ppermute x6, waiting for transfers between devices, local(): arrived = lax.ppermute(outgoing.astype(jnp.bfloat16), 'peer', pairs)  34.2 us
    all_to_all x1, waiting for transfers between devices, local(): lax.all_to_all(grad_rows.reshape(micro_count, batch_rows, feature_count),...  16.6 us
    ppermute x6, starting transfers between devices, local(): arrived = lax.ppermute(outgoing.astype(jnp.bfloat16), 'peer', pairs)  16.1 us
  transfers between devices with their start and end apart: 21, of which 9 were waited for; matrix products, arithmetic and copies ran while one was open for 1% of the time, Pallas kernels for 0%

profile of v4, /device:TPU:6, one launch (start us, length us, event | category | flops | bytes accessed | tf_op | source)
XLA Modules:
  0.0 742.1 jit_solution(11038497742604960156)
XLA Ops:
  8.3 33.1 %all_to_all.70 = bf16[2,64,2560]{2,0,1:T(2,128)(2,1)S(1)} all-to-all(bf16[2,64,2560]{2,0,1:T(2,128)(2,1)S(1)} %copy.111), channel_id=1, replica_groups=mesh['section'=8,'peer'=64] {'peer'}, dimensions={1} | all-to-all | bytes 1310720 | tf_op jit(solution)/shard_map/all_to_all | solution.py:94
  41.5 3.5 collective-permute-start
  45.0 14.9 %collective-permute-done = bf16[2,64,2560]{2,1,0:T(8,128)(2,1)S(1)} collective-permute-done((bf16[2,64,2560]{2,1,0:T(8,128)(2,1)S(1)}, bf16[2,64,2560]{2,1,0:T(8,128)(2,1)S(1)}, u32[]{:S(2)}, u32[]{:S(2)}) %collective-permute-start) | collective-permute-done | bytes 655392 | tf_op jit(solution)/shard_map/ppermute | solution.py:95
  62.4 25.2 %all_to_all.71 = bf16[2,64,2560]{2,0,1:T(2,128)(2,1)S(1)} all-to-all(bf16[2,64,2560]{2,0,1:T(2,128)(2,1)S(1)} %copy.113), channel_id=1, replica_groups=mesh['section'=8,'peer'=64] {'peer'}, dimensions={1} | all-to-all | bytes 1310720 | tf_op jit(solution)/shard_map/all_to_all | solution.py:94
  90.9 26.2 %all_to_all.72 = bf16[2,64,2560]{2,0,1:T(2,128)(2,1)S(1)} all-to-all(bf16[2,64,2560]{2,0,1:T(2,128)(2,1)S(1)} %copy.115), channel_id=1, replica_groups=mesh['section'=8,'peer'=64] {'peer'}, dimensions={1} | all-to-all | bytes 1310720 | tf_op jit(solution)/shard_map/all_to_all | solution.py:94
  120.4 26.2 %all_to_all.73 = bf16[2,64,2560]{2,0,1:T(2,128)(2,1)S(1)} all-to-all(bf16[2,64,2560]{2,0,1:T(2,128)(2,1)S(1)} %copy.117), channel_id=1, replica_groups=mesh['section'=8,'peer'=64] {'peer'}, dimensions={1} | all-to-all | bytes 1310720 | tf_op jit(solution)/shard_map/all_to_all | solution.py:94
  149.9 26.2 %all_to_all.74 = bf16[2,64,2560]{2,0,1:T(2,128)(2,1)S(1)} all-to-all(bf16[2,64,2560]{2,0,1:T(2,128)(2,1)S(1)} %copy.119), channel_id=1, replica_groups=mesh['section'=8,'peer'=64] {'peer'}, dimensions={1} | all-to-all | bytes 1310720 | tf_op jit(solution)/shard_map/all_to_all | solution.py:94
  179.4 26.2 %all_to_all.75 = bf16[2,64,2560]{2,0,1:T(2,128)(2,1)S(1)} all-to-all(bf16[2,64,2560]{2,0,1:T(2,128)(2,1)S(1)} %copy.121), channel_id=1, replica_groups=mesh['section'=8,'peer'=64] {'peer'}, dimensions={1} | all-to-all | bytes 1310720 | tf_op jit(solution)/shard_map/all_to_all | solution.py:94
  208.9 26.2 %all_to_all.76 = bf16[2,64,2560]{2,0,1:T(2,128)(2,1)S(1)} all-to-all(bf16[2,64,2560]{2,0,1:T(2,128)(2,1)S(1)} %copy.123), channel_id=1, replica_groups=mesh['section'=8,'peer'=64] {'peer'}, dimensions={1} | all-to-all | bytes 1310720 | tf_op jit(solution)/shard_map/all_to_all | solution.py:94
  250.3 26.2 %all_to_all.77 = bf16[2,64,2560]{2,0,1:T(2,128)(2,1)S(1)} all-to-all(bf16[2,64,2560]{2,0,1:T(2,128)(2,1)S(1)} %copy.125), channel_id=1, replica_groups=mesh['section'=8,'peer'=64] {'peer'}, dimensions={1} | all-to-all | bytes 1310720 | tf_op jit(solution)/shard_map/all_to_all | solution.py:115
  280.4 26.2 %all_to_all.78 = bf16[2,64,2560]{2,0,1:T(2,128)(2,1)S(1)} all-to-all(bf16[2,64,2560]{2,0,1:T(2,128)(2,1)S(1)} %copy.128), channel_id=1, replica_groups=mesh['section'=8,'peer'=64] {'peer'}, dimensions={1} | all-to-all | bytes 1310720 | tf_op jit(solution)/shard_map/all_to_all | solution.py:115
  310.7 26.1 %all_to_all.79 = bf16[2,64,2560]{2,0,1:T(2,128)(2,1)S(1)} all-to-all(bf16[2,64,2560]{2,0,1:T(2,128)(2,1)S(1)} %copy.131), channel_id=1, replica_groups=mesh['section'=8,'peer'=64] {'peer'}, dimensions={1} | all-to-all | bytes 1310720 | tf_op jit(solution)/shard_map/all_to_all | solution.py:115
  341.1 26.2 %all_to_all.80 = bf16[2,64,2560]{2,0,1:T(2,128)(2,1)S(1)} all-to-all(bf16[2,64,2560]{2,0,1:T(2,128)(2,1)S(1)} %copy.134), channel_id=1, replica_groups=mesh['section'=8,'peer'=64] {'peer'}, dimensions={1} | all-to-all | bytes 1310720 | tf_op jit(solution)/shard_map/all_to_all | solution.py:115
  371.4 26.2 %all_to_all.81 = bf16[2,64,2560]{2,0,1:T(2,128)(2,1)S(1)} all-to-all(bf16[2,64,2560]{2,0,1:T(2,128)(2,1)S(1)} %copy.137), channel_id=1, replica_groups=mesh['section'=8,'peer'=64] {'peer'}, dimensions={1} | all-to-all | bytes 1310720 | tf_op jit(solution)/shard_map/all_to_all | solution.py:115
  401.6 26.1 %all_to_all.82 = bf16[2,64,2560]{2,0,1:T(2,128)(2,1)S(1)} all-to-all(bf16[2,64,2560]{2,0,1:T(2,128)(2,1)S(1)} %copy.140), channel_id=1, replica_groups=mesh['section'=8,'peer'=64] {'peer'}, dimensions={1} | all-to-all | bytes 1310720 | tf_op jit(solution)/shard_map/all_to_all | solution.py:115
  432.7 7.2 all-to-all-start.13
  442.6 16.6 %all-to-all-done.13 = bf16[2,64,2560]{2,0,1:T(2,128)(2,1)} async-done(((bf16[2,64,2560]{2,0,1:T(2,128)(2,1)}), bf16[2,64,2560]{2,0,1:T(2,128)(2,1)}, u32[]{:S(2)}, u32[]{:S(2)}) %all-to-all-start.13) | async-done | bytes 655392 | tf_op jit(solution)/shard_map/all_to_all | solution.py:115
  461.8 5.1 fusion.141
  467.0 208.6 %collective-permute-done.13 = bf16[2,64,2560]{2,1,0:T(8,128)(2,1)S(1)} collective-permute-done((bf16[2,64,2560]{2,1,0:T(8,128)(2,1)S(1)}, bf16[2,64,2560]{2,1,0:T(8,128)(2,1)S(1)}, u32[]{:S(2)}, u32[]{:S(2)}) %collective-permute-start.13) | collective-permute-done | bytes 655392 | tf_op jit(solution)/shard_map/ppermute | solution.py:118
  694.5 8.3 %collective-permute-done.15 = bf16[96,2560]{1,0:T(8,128)(2,1)} collective-permute-done((bf16[96,2560]{1,0:T(8,128)(2,1)}, bf16[96,2560]{1,0:T(8,128)(2,1)}, u32[]{:S(2)}, u32[]{:S(2)}) %collective-permute-start.15) | collective-permute-done | bytes 491552 | tf_op jit(solution)/shard_map/ppermute | solution.py:157
  707.6 5.4 collective-permute-done.16
  716.6 6.5 collective-permute-done.17
  726.4 4.6 collective-permute-done.18
  734.2 6.7 collective-permute-done.19
  (325 shorter events, 106.2 us)
Async XLA Ops:
  41.5 18.4 %collective-permute-start = (bf16[2,64,2560]{2,1,0:T(8,128)(2,1)S(1)}, bf16[2,64,2560]{2,1,0:T(8,128)(2,1)S(1)}, u32[]{:S(2)}, u32[]{:S(2)}) collective-permute-start(bf16[2,64,2560]{2,1,0:T(8,128)(2,1)S(1)} %copy.112), channel_id=1, source_target_pairs={{0,64},{1,65},{2,66},{3,67},{4,68},{5,69},{6,70},{7,71},{8,72},{9,... | collective-permute-start | bytes 1966088 | tf_op jit(solution)/shard_map/ppermute | solution.py:95
  87.7 0.7 collective-permute-start.1
  117.2 0.7 collective-permute-start.2
  146.7 0.7 collective-permute-start.3
  176.1 0.7 collective-permute-start.4
  205.6 0.7 collective-permute-start.5
  235.9 2.3 collective-permute-start.6
  276.6 0.7 collective-permute-start.7
  306.7 0.7 collective-permute-start.8
  336.9 0.9 collective-permute-start.9
  367.4 0.7 collective-permute-start.10
  397.6 0.7 collective-permute-start.11
  427.9 0.7 collective-permute-start.12
  432.7 26.5 %all-to-all-start.13 = ((bf16[2,64,2560]{2,0,1:T(2,128)(2,1)}), bf16[2,64,2560]{2,0,1:T(2,128)(2,1)}, u32[]{:S(2)}, u32[]{:S(2)}) async-start(bf16[2,64,2560]{2,0,1:T(2,128)(2,1)} %copy.143), calls=%async_computation.13 | async-start | bytes 1310720 | tf_op jit(solution)/shard_map/all_to_all | solution.py:115
  460.5 215.0 %collective-permute-start.13 = (bf16[2,64,2560]{2,1,0:T(8,128)(2,1)S(1)}, bf16[2,64,2560]{2,1,0:T(8,128)(2,1)S(1)}, u32[]{:S(2)}, u32[]{:S(2)}) collective-permute-start(bf16[2,64,2560]{2,1,0:T(8,128)(2,1)S(1)} %copy.144), channel_id=1, source_target_pairs={{64,0},{65,1},{66,2},{67,3},{68,4},{69,5},{70,6},{71,7},{72,8},{73... | collective-permute-start | bytes 1966088 | tf_op jit(solution)/shard_map/ppermute | solution.py:118
  461.8 214.8 %copy-start.18 = (bf16[2,64,2560]{2,1,0:T(8,128)(2,1)S(1)}, bf16[2,64,2560]{2,1,0:T(8,128)(2,1)}, u32[]{:S(2)}) copy-start(bf16[2,64,2560]{2,1,0:T(8,128)(2,1)} %copy-done.17) | copy-start | bytes 1966084
  461.8 214.8 %copy-start.20 = (bf16[2,64,2560]{2,1,0:T(8,128)(2,1)S(1)}, bf16[2,64,2560]{2,1,0:T(8,128)(2,1)}, u32[]{:S(2)}) copy-start(bf16[2,64,2560]{2,1,0:T(8,128)(2,1)} %copy-done.19) | copy-start | bytes 1966084
  461.8 214.8 %copy-start.22 = (bf16[2,64,2560]{2,1,0:T(8,128)(2,1)S(1)}, bf16[2,64,2560]{2,1,0:T(8,128)(2,1)}, u32[]{:S(2)}) copy-start(bf16[2,64,2560]{2,1,0:T(8,128)(2,1)} %copy-done.21) | copy-start | bytes 1966084
  684.3 4.6 collective-permute-start.14
  691.8 11.0 %collective-permute-start.15 = (bf16[96,2560]{1,0:T(8,128)(2,1)}, bf16[96,2560]{1,0:T(8,128)(2,1)}, u32[]{:S(2)}, u32[]{:S(2)}) collective-permute-start(bf16[96,2560]{1,0:T(8,128)(2,1)} %dynamic-slice_convert_fusion.1), channel_id=1, source_target_pairs={{0,2},{1,17},{2,0},{3,19},{4,6},{5,21},{6,4},{7,23},{8,10},{9,25},... | collective-permute-start | bytes 1474568 | tf_op jit(solution)/shard_map/ppermute | solution.py:157
  705.0 8.1 %collective-permute-start.16 = (bf16[48,2560]{1,0:T(8,128)(2,1)S(1)}, bf16[48,2560]{1,0:T(8,128)(2,1)S(1)}, u32[]{:S(2)}, u32[]{:S(2)}) collective-permute-start(bf16[48,2560]{1,0:T(8,128)(2,1)S(1)} %dynamic-slice_convert_fusion.2), channel_id=1, source_target_pairs={{0,16},{1,3},{2,18},{3,1},{4,20},{5,7},{6,22},{7,5},{8,24},{9,11},... | collective-permute-start | bytes 737288 | tf_op jit(solution)/shard_map/ppermute | solution.py:157
  714.2 9.0 %collective-permute-start.17 = (bf16[24,2560]{1,0:T(8,128)(2,1)S(1)}, bf16[24,2560]{1,0:T(8,128)(2,1)S(1)}, u32[]{:S(2)}, u32[]{:S(2)}) collective-permute-start(bf16[24,2560]{1,0:T(8,128)(2,1)S(1)} %dynamic-slice_convert_fusion.3), channel_id=1, source_target_pairs={{0,4},{1,33},{2,6},{3,35},{4,0},{5,37},{6,2},{7,39},{8,12},{9,41},... | collective-permute-start | bytes 368648 | tf_op jit(solution)/shard_map/ppermute | solution.py:157
  723.2 7.8 %collective-permute-start.18 = (bf16[12,2560]{1,0:T(8,128)(2,1)S(1)}, bf16[12,2560]{1,0:T(8,128)(2,1)S(1)}, u32[]{:S(2)}, u32[]{:S(2)}) collective-permute-start(bf16[12,2560]{1,0:T(8,128)(2,1)S(1)} %dynamic-slice_convert_fusion.4), channel_id=1, source_target_pairs={{0,32},{1,5},{2,34},{3,7},{4,36},{5,1},{6,38},{7,3},{8,40},{9,13},... | collective-permute-start | bytes 184328 | tf_op jit(solution)/shard_map/ppermute | solution.py:157
  731.1 9.8 %collective-permute-start.19 = (bf16[6,2560]{1,0:T(8,128)(2,1)S(1)}, bf16[6,2560]{1,0:T(8,128)(2,1)S(1)}, u32[]{:S(2)}, u32[]{:S(2)}) collective-permute-start(bf16[6,2560]{1,0:T(8,128)(2,1)S(1)} %dynamic-slice_convert_fusion.5), channel_id=1, source_target_pairs={{0,8},{1,9},{2,10},{3,11},{4,12},{5,13},{6,14},{7,15},{8,0},{9,1},... | collective-permute-start | bytes 92168 | tf_op jit(solution)/shard_map/ppermute | solution.py:157
  (65 other events, 1202.0 us)

commit v5 on v4

--- a/solution.py
+++ b/solution.py
@@ -88,11 +88,15 @@
         keep_active = jnp.where(mine, active, keep_active)
         keep_slope = jnp.where(mine, gelu_slope, keep_slope)
         if k < sections - 1:
-            packed = permute_rows(
-                send_onehot[k], outputs.reshape(micro_count, batch_rows, feature_count), "mdq,mqf->mdf"
-            )
+            blocks = outputs.reshape(micro_count, batch_rows, feature_count)
+            half = feature_count // 2
+            raw_later = lax.ppermute(blocks[:, :, half:], "section", [(k, k + 1)])
+            packed = permute_rows(send_onehot[k], blocks[:, :, :half], "mdq,mqf->mdf")
             received = lax.all_to_all(packed, "peer", 1, 1, tiled=True)
-            x = lax.ppermute(received, "section", [(k, k + 1)])
+            moved = lax.ppermute(received, "section", [(k, k + 1)])
+            packed_later = permute_rows(send_onehot[k], raw_later, "mdq,mqf->mdf")
+            received_later = lax.all_to_all(packed_later, "peer", 1, 1, tiled=True)
+            x = jnp.concatenate([moved, received_later], axis=2)
         else:
             upstream = outputs
 
@@ -112,13 +116,15 @@
         keep_upstream = jnp.where(mine, upstream, keep_upstream)
         keep_grad_hidden = jnp.where(mine, grad_hidden, keep_grad_hidden)
         if k > 0:
-            sent = lax.all_to_all(
-                grad_rows.reshape(micro_count, batch_rows, feature_count), "peer", 1, 1, tiled=True
-            )
+            blocks = grad_rows.reshape(micro_count, batch_rows, feature_count)
+            half = feature_count // 2
+            raw_later = lax.ppermute(blocks[:, :, half:], "section", [(k, k - 1)])
+            sent = lax.all_to_all(blocks[:, :, :half], "peer", 1, 1, tiled=True)
             moved = lax.ppermute(sent, "section", [(k, k - 1)])
-            upstream = permute_rows(send_onehot[k - 1], moved, "mdq,mdf->mqf").reshape(
-                row_count, feature_count
-            )
+            sent_later = lax.all_to_all(raw_later, "peer", 1, 1, tiled=True)
+            upstream = permute_rows(
+                send_onehot[k - 1], jnp.concatenate([moved, sent_later], axis=2), "mdq,mdf->mqf"
+            ).reshape(row_count, feature_count)
 
     bits_count = peer_count.bit_length() - 1
     peers = jnp.arange(peer_count, dtype=jnp.int32)

time: 752 us -> 813 us (1.081)
  blocking collectives: 346 us -> 0 us
  starting transfers between devices: 37.8 us -> 262 us
  waiting for transfers between devices: 274 us -> 385 us
  local copies, waits for them, and re-layouts: 29.7 us -> 94.6 us
    all_to_all x13 -> x0, blocking collectives: 346 us -> none  [the longest x7 189 us: local(): received = lax.all_to_all(packed, 'peer', 1, 1, tiled=True)]
    all_to_all x1 -> x28, waiting for transfers between devices: 16.6 us -> 258 us  [the longest x7 70.8 us: local(): received_later = lax.all_to_all(packed_later, 'peer', 1, 1, tiled=True)]
    ppermute x7, waiting for transfers between devices: 209 us -> 0.02 us  [local(): moved = lax.ppermute(sent, 'section', [(k, k - 1)])]
    all_to_all x1 -> x28, starting transfers between devices: 7.23 us -> 203 us  [the longest x7 56.3 us: local(): received = lax.all_to_all(packed, 'peer', 1, 1, tiled=True)]
    ppermute x7 -> x21, waiting for transfers between devices: 14.9 us -> 99.2 us  [the longest x7 84.4 us: local(): raw_later = lax.ppermute(blocks[:, :, half:], 'section', [(k, k - 1)])]
    unnamed x138 -> x212, local copies, waits for them, and re-layouts: 8.63 us -> 32.3 us
    all_to_all x14 -> x21, local copies, waits for them, and re-layouts: 2.95 us -> 25.5 us  [the longest x7 12.2 us: local(): sent = lax.all_to_all(blocks[:, :, :half], 'peer', 1, 1, tiled=True)]
    ppermute x7 -> x21, starting transfers between devices: 8.83 us -> 26.7 us  [the longest x7 9.73 us: local(): raw_later = lax.ppermute(blocks[:, :, half:], 'section', [(k, k - 1)])]
  transfers between devices with their start and end apart: 21 -> 62, of which waited for: 9 -> 36; matrix products, arithmetic and copies ran while one was open for 1% -> 6% of each run, Pallas kernels for 0% -> 0%
where the time goes in v5:
time: 813 us; the launch traced here: 802 us
  waiting for transfers between devices  385 us (47%)
  starting transfers between devices  262 us (32%)
  local copies, waits for them, and re-layouts  94.6 us (12%)
  matrix products  32.2 us (4%)
  other arithmetic  26 us (3%)
    ppermute x7, waiting for transfers between devices, local(): raw_later = lax.ppermute(blocks[:, :, half:], 'section', [(k, k - 1)])  84.4 us
    all_to_all x7, waiting for transfers between devices, local(): received_later = lax.all_to_all(packed_later, 'peer', 1, 1, tiled=True)  70.8 us
    all_to_all x7, waiting for transfers between devices, local(): received = lax.all_to_all(packed, 'peer', 1, 1, tiled=True)  65.8 us
    all_to_all x7, waiting for transfers between devices, local(): sent_later = lax.all_to_all(raw_later, 'peer', 1, 1, tiled=True)  60.6 us
    all_to_all x7, waiting for transfers between devices, local(): sent = lax.all_to_all(blocks[:, :, :half], 'peer', 1, 1, tiled=True)  60.5 us
    all_to_all x7, starting transfers between devices, local(): received = lax.all_to_all(packed, 'peer', 1, 1, tiled=True)  56.3 us
    all_to_all x7, starting transfers between devices, local(): sent_later = lax.all_to_all(raw_later, 'peer', 1, 1, tiled=True)  51.1 us
    all_to_all x7, starting transfers between devices, local(): received_later = lax.all_to_all(packed_later, 'peer', 1, 1, tiled=True)  48.7 us
  transfers between devices with their start and end apart: 62, of which 36 were waited for; matrix products, arithmetic and copies ran while one was open for 6% of the time, Pallas kernels for 0%

profile of v5, /device:TPU:6, one launch (start us, length us, event | category | flops | bytes accessed | tf_op | source)
XLA Modules:
  0.0 801.7 jit_solution(2109454369779103509)
XLA Ops:
  8.3 14.0 %all-to-all-start = ((bf16[2,64,1280]{2,0,1:T(2,128)(2,1)}), bf16[2,64,1280]{2,0,1:T(2,128)(2,1)S(1)}, u32[]{:S(2)}, u32[]{:S(2)}) async-start(bf16[2,64,1280]{2,0,1:T(2,128)(2,1)} %copy.261), calls=%async_computation | async-start | bytes 655360 | tf_op jit(solution)/shard_map/all_to_all | solution.py:95
  76.0 10.8 %all-to-all-done.2 = bf16[2,64,1280]{2,0,1:T(2,128)(2,1)S(1)} async-done(((bf16[2,64,1280]{2,0,1:T(2,128)(2,1)}), bf16[2,64,1280]{2,0,1:T(2,128)(2,1)S(1)}, u32[]{:S(2)}, u32[]{:S(2)}) %all-to-all-start.2) | async-done | bytes 327712 | tf_op jit(solution)/shard_map/all_to_all | solution.py:95
  96.3 10.7 %all-to-all-done.3 = bf16[2,64,1280]{2,0,1:T(2,128)(2,1)S(1)} async-done(((bf16[2,64,1280]{2,0,1:T(2,128)(2,1)}), bf16[2,64,1280]{2,0,1:T(2,128)(2,1)S(1)}, u32[]{:S(2)}, u32[]{:S(2)}) %all-to-all-start.3) | async-done | bytes 327712 | tf_op jit(solution)/shard_map/all_to_all | solution.py:98
  121.5 10.8 %all-to-all-done.4 = bf16[2,64,1280]{2,0,1:T(2,128)(2,1)S(1)} async-done(((bf16[2,64,1280]{2,0,1:T(2,128)(2,1)}), bf16[2,64,1280]{2,0,1:T(2,128)(2,1)S(1)}, u32[]{:S(2)}, u32[]{:S(2)}) %all-to-all-start.4) | async-done | bytes 327712 | tf_op jit(solution)/shard_map/all_to_all | solution.py:95
  139.6 12.2 %all-to-all-done.5 = bf16[2,64,1280]{2,0,1:T(2,128)(2,1)S(1)} async-done(((bf16[2,64,1280]{2,0,1:T(2,128)(2,1)}), bf16[2,64,1280]{2,0,1:T(2,128)(2,1)S(1)}, u32[]{:S(2)}, u32[]{:S(2)}) %all-to-all-start.5) | async-done | bytes 327712 | tf_op jit(solution)/shard_map/all_to_all | solution.py:98
  164.3 10.8 %all-to-all-done.6 = bf16[2,64,1280]{2,0,1:T(2,128)(2,1)S(1)} async-done(((bf16[2,64,1280]{2,0,1:T(2,128)(2,1)}), bf16[2,64,1280]{2,0,1:T(2,128)(2,1)S(1)}, u32[]{:S(2)}, u32[]{:S(2)}) %all-to-all-start.6) | async-done | bytes 327712 | tf_op jit(solution)/shard_map/all_to_all | solution.py:95
  183.5 11.7 %all-to-all-done.7 = bf16[2,64,1280]{2,0,1:T(2,128)(2,1)S(1)} async-done(((bf16[2,64,1280]{2,0,1:T(2,128)(2,1)}), bf16[2,64,1280]{2,0,1:T(2,128)(2,1)S(1)}, u32[]{:S(2)}, u32[]{:S(2)}) %all-to-all-start.7) | async-done | bytes 327712 | tf_op jit(solution)/shard_map/all_to_all | solution.py:98
  209.8 10.8 %all-to-all-done.8 = bf16[2,64,1280]{2,0,1:T(2,128)(2,1)S(1)} async-done(((bf16[2,64,1280]{2,0,1:T(2,128)(2,1)}), bf16[2,64,1280]{2,0,1:T(2,128)(2,1)S(1)}, u32[]{:S(2)}, u32[]{:S(2)}) %all-to-all-start.8) | async-done | bytes 327712 | tf_op jit(solution)/shard_map/all_to_all | solution.py:95
  228.9 11.9 %all-to-all-done.9 = bf16[2,64,1280]{2,0,1:T(2,128)(2,1)S(1)} async-done(((bf16[2,64,1280]{2,0,1:T(2,128)(2,1)}), bf16[2,64,1280]{2,0,1:T(2,128)(2,1)S(1)}, u32[]{:S(2)}, u32[]{:S(2)}) %all-to-all-start.9) | async-done | bytes 327712 | tf_op jit(solution)/shard_map/all_to_all | solution.py:98
  255.4 10.8 %all-to-all-done.10 = bf16[2,64,1280]{2,0,1:T(2,128)(2,1)S(1)} async-done(((bf16[2,64,1280]{2,0,1:T(2,128)(2,1)}), bf16[2,64,1280]{2,0,1:T(2,128)(2,1)S(1)}, u32[]{:S(2)}, u32[]{:S(2)}) %all-to-all-start.10) | async-done | bytes 327712 | tf_op jit(solution)/shard_map/all_to_all | solution.py:95
  274.6 11.7 %all-to-all-done.11 = bf16[2,64,1280]{2,0,1:T(2,128)(2,1)S(1)} async-done(((bf16[2,64,1280]{2,0,1:T(2,128)(2,1)}), bf16[2,64,1280]{2,0,1:T(2,128)(2,1)S(1)}, u32[]{:S(2)}, u32[]{:S(2)}) %all-to-all-start.11) | async-done | bytes 327712 | tf_op jit(solution)/shard_map/all_to_all | solution.py:98
  301.0 10.8 %all-to-all-done.12 = bf16[2,64,1280]{2,0,1:T(2,128)(2,1)S(1)} async-done(((bf16[2,64,1280]{2,0,1:T(2,128)(2,1)}), bf16[2,64,1280]{2,0,1:T(2,128)(2,1)S(1)}, u32[]{:S(2)}, u32[]{:S(2)}) %all-to-all-start.12) | async-done | bytes 327712 | tf_op jit(solution)/shard_map/all_to_all | solution.py:95
  319.3 11.9 %all-to-all-done.13 = bf16[2,64,1280]{2,0,1:T(2,128)(2,1)S(1)} async-done(((bf16[2,64,1280]{2,0,1:T(2,128)(2,1)}), bf16[2,64,1280]{2,0,1:T(2,128)(2,1)S(1)}, u32[]{:S(2)}, u32[]{:S(2)}) %all-to-all-start.13) | async-done | bytes 327712 | tf_op jit(solution)/shard_map/all_to_all | solution.py:98
  353.7 10.1 %all-to-all-done.14 = bf16[2,64,1280]{2,0,1:T(2,128)(2,1)} async-done(((bf16[2,64,1280]{2,0,1:T(2,128)(2,1)}), bf16[2,64,1280]{2,0,1:T(2,128)(2,1)}, u32[]{:S(2)}, u32[]{:S(2)}) %all-to-all-start.14) | async-done | bytes 327712 | tf_op jit(solution)/shard_map/all_to_all | solution.py:122
  374.0 9.7 %all-to-all-done.15 = bf16[2,64,1280]{2,0,1:T(2,128)(2,1)} async-done(((bf16[2,64,1280]{2,0,1:T(2,128)(2,1)}), bf16[2,64,1280]{2,0,1:T(2,128)(2,1)}, u32[]{:S(2)}, u32[]{:S(2)}) %all-to-all-start.15) | async-done | bytes 327712 | tf_op jit(solution)/shard_map/all_to_all | solution.py:124
  398.7 10.1 %all-to-all-done.16 = bf16[2,64,1280]{2,0,1:T(2,128)(2,1)} async-done(((bf16[2,64,1280]{2,0,1:T(2,128)(2,1)}), bf16[2,64,1280]{2,0,1:T(2,128)(2,1)}, u32[]{:S(2)}, u32[]{:S(2)}) %all-to-all-start.16) | async-done | bytes 327712 | tf_op jit(solution)/shard_map/all_to_all | solution.py:122
  418.6 9.7 %all-to-all-done.17 = bf16[2,64,1280]{2,0,1:T(2,128)(2,1)} async-done(((bf16[2,64,1280]{2,0,1:T(2,128)(2,1)}), bf16[2,64,1280]{2,0,1:T(2,128)(2,1)}, u32[]{:S(2)}, u32[]{:S(2)}) %all-to-all-start.17) | async-done | bytes 327712 | tf_op jit(solution)/shard_map/all_to_all | solution.py:124
  443.6 10.1 %all-to-all-done.18 = bf16[2,64,1280]{2,0,1:T(2,128)(2,1)} async-done(((bf16[2,64,1280]{2,0,1:T(2,128)(2,1)}), bf16[2,64,1280]{2,0,1:T(2,128)(2,1)}, u32[]{:S(2)}, u32[]{:S(2)}) %all-to-all-start.18) | async-done | bytes 327712 | tf_op jit(solution)/shard_map/all_to_all | solution.py:122
  488.4 10.1 %all-to-all-done.20 = bf16[2,64,1280]{2,0,1:T(2,128)(2,1)} async-done(((bf16[2,64,1280]{2,0,1:T(2,128)(2,1)}), bf16[2,64,1280]{2,0,1:T(2,128)(2,1)}, u32[]{:S(2)}, u32[]{:S(2)}) %all-to-all-start.20) | async-done | bytes 327712 | tf_op jit(solution)/shard_map/all_to_all | solution.py:122
  533.1 10.1 %all-to-all-done.22 = bf16[2,64,1280]{2,0,1:T(2,128)(2,1)} async-done(((bf16[2,64,1280]{2,0,1:T(2,128)(2,1)}), bf16[2,64,1280]{2,0,1:T(2,128)(2,1)}, u32[]{:S(2)}, u32[]{:S(2)}) %all-to-all-start.22) | async-done | bytes 327712 | tf_op jit(solution)/shard_map/all_to_all | solution.py:122
  553.0 9.7 %all-to-all-done.23 = bf16[2,64,1280]{2,0,1:T(2,128)(2,1)} async-done(((bf16[2,64,1280]{2,0,1:T(2,128)(2,1)}), bf16[2,64,1280]{2,0,1:T(2,128)(2,1)}, u32[]{:S(2)}, u32[]{:S(2)}) %all-to-all-start.23) | async-done | bytes 327712 | tf_op jit(solution)/shard_map/all_to_all | solution.py:124
  577.8 10.1 %all-to-all-done.24 = bf16[2,64,1280]{2,0,1:T(2,128)(2,1)} async-done(((bf16[2,64,1280]{2,0,1:T(2,128)(2,1)}), bf16[2,64,1280]{2,0,1:T(2,128)(2,1)}, u32[]{:S(2)}, u32[]{:S(2)}) %all-to-all-start.24) | async-done | bytes 327712 | tf_op jit(solution)/shard_map/all_to_all | solution.py:122
  627.0 84.4 %collective-permute-done.27 = bf16[2,64,1280]{2,0,1:T(2,128)(2,1)} collective-permute-done((bf16[2,64,1280]{2,0,1:T(2,128)(2,1)S(1)}, bf16[2,64,1280]{2,0,1:T(2,128)(2,1)}, u32[]{:S(2)}, u32[]{:S(2)}) %collective-permute-start.27) | collective-permute-done | bytes 327712 | tf_op jit(solution)/shard_map/ppermute | solution.py:121
  711.4 10.5 %all-to-all-start.27 = ((bf16[2,64,1280]{2,0,1:T(2,128)(2,1)}), bf16[2,64,1280]{2,0,1:T(2,128)(2,1)}, u32[]{:S(2)}, u32[]{:S(2)}) async-start(bf16[2,64,1280]{2,0,1:T(2,128)(2,1)} %collective-permute-done.27), calls=%async_computation.27 | async-start | bytes 655360 | tf_op jit(solution)/shard_map/all_to_all | solution.py:124
  (510 shorter events, 465.5 us)
Async XLA Ops:
  8.3 26.9 %all-to-all-start = ((bf16[2,64,1280]{2,0,1:T(2,128)(2,1)}), bf16[2,64,1280]{2,0,1:T(2,128)(2,1)S(1)}, u32[]{:S(2)}, u32[]{:S(2)}) async-start(bf16[2,64,1280]{2,0,1:T(2,128)(2,1)} %copy.261), calls=%async_computation | async-start | bytes 655360 | tf_op jit(solution)/shard_map/all_to_all | solution.py:95
  35.9 22.4 %all-to-all-start.1 = ((bf16[2,64,1280]{2,0,1:T(2,128)(2,1)}), bf16[2,64,1280]{2,0,1:T(2,128)(2,1)S(1)}, u32[]{:S(2)}, u32[]{:S(2)}) async-start(bf16[2,64,1280]{2,0,1:T(2,128)(2,1)} %copy.262), calls=%async_computation.1 | async-start | bytes 655360 | tf_op jit(solution)/shard_map/all_to_all | solution.py:98
  64.3 22.5 %all-to-all-start.2 = ((bf16[2,64,1280]{2,0,1:T(2,128)(2,1)}), bf16[2,64,1280]{2,0,1:T(2,128)(2,1)S(1)}, u32[]{:S(2)}, u32[]{:S(2)}) async-start(bf16[2,64,1280]{2,0,1:T(2,128)(2,1)} %copy.267), calls=%async_computation.2 | async-start | bytes 655360 | tf_op jit(solution)/shard_map/all_to_all | solution.py:95
  87.6 19.4 %all-to-all-start.3 = ((bf16[2,64,1280]{2,0,1:T(2,128)(2,1)}), bf16[2,64,1280]{2,0,1:T(2,128)(2,1)S(1)}, u32[]{:S(2)}, u32[]{:S(2)}) async-start(bf16[2,64,1280]{2,0,1:T(2,128)(2,1)} %copy.268), calls=%async_computation.3 | async-start | bytes 655360 | tf_op jit(solution)/shard_map/all_to_all | solution.py:98
  113.0 19.4 %all-to-all-start.4 = ((bf16[2,64,1280]{2,0,1:T(2,128)(2,1)}), bf16[2,64,1280]{2,0,1:T(2,128)(2,1)S(1)}, u32[]{:S(2)}, u32[]{:S(2)}) async-start(bf16[2,64,1280]{2,0,1:T(2,128)(2,1)} %copy.273), calls=%async_computation.4 | async-start | bytes 655360 | tf_op jit(solution)/shard_map/all_to_all | solution.py:95
  132.4 19.4 %all-to-all-start.5 = ((bf16[2,64,1280]{2,0,1:T(2,128)(2,1)}), bf16[2,64,1280]{2,0,1:T(2,128)(2,1)S(1)}, u32[]{:S(2)}, u32[]{:S(2)}) async-start(bf16[2,64,1280]{2,0,1:T(2,128)(2,1)} %copy.274), calls=%async_computation.5 | async-start | bytes 655360 | tf_op jit(solution)/shard_map/all_to_all | solution.py:98
  155.7 19.4 %all-to-all-start.6 = ((bf16[2,64,1280]{2,0,1:T(2,128)(2,1)}), bf16[2,64,1280]{2,0,1:T(2,128)(2,1)S(1)}, u32[]{:S(2)}, u32[]{:S(2)}) async-start(bf16[2,64,1280]{2,0,1:T(2,128)(2,1)} %copy.279), calls=%async_computation.6 | async-start | bytes 655360 | tf_op jit(solution)/shard_map/all_to_all | solution.py:95
  175.8 19.4 %all-to-all-start.7 = ((bf16[2,64,1280]{2,0,1:T(2,128)(2,1)}), bf16[2,64,1280]{2,0,1:T(2,128)(2,1)S(1)}, u32[]{:S(2)}, u32[]{:S(2)}) async-start(bf16[2,64,1280]{2,0,1:T(2,128)(2,1)} %copy.280), calls=%async_computation.7 | async-start | bytes 655360 | tf_op jit(solution)/shard_map/all_to_all | solution.py:98
  311.8 19.4 %all-to-all-start.13 = ((bf16[2,64,1280]{2,0,1:T(2,128)(2,1)}), bf16[2,64,1280]{2,0,1:T(2,128)(2,1)S(1)}, u32[]{:S(2)}, u32[]{:S(2)}) async-start(bf16[2,64,1280]{2,0,1:T(2,128)(2,1)} %copy.298), calls=%async_computation.13 | async-start | bytes 655360 | tf_op jit(solution)/shard_map/all_to_all | solution.py:98
  344.3 19.5 %all-to-all-start.14 = ((bf16[2,64,1280]{2,0,1:T(2,128)(2,1)}), bf16[2,64,1280]{2,0,1:T(2,128)(2,1)}, u32[]{:S(2)}, u32[]{:S(2)}) async-start(bf16[2,64,1280]{2,0,1:T(2,128)(2,1)} %copy.348), calls=%async_computation.14 | async-start | bytes 655360 | tf_op jit(solution)/shard_map/all_to_all | solution.py:122
  363.7 19.9 %all-to-all-start.15 = ((bf16[2,64,1280]{2,0,1:T(2,128)(2,1)}), bf16[2,64,1280]{2,0,1:T(2,128)(2,1)}, u32[]{:S(2)}, u32[]{:S(2)}) async-start(bf16[2,64,1280]{2,0,1:T(2,128)(2,1)} %collective-permute-done.15), calls=%async_computation.15 | async-start | bytes 655360 | tf_op jit(solution)/shard_map/all_to_all | solution.py:124
  389.3 19.5 %all-to-all-start.16 = ((bf16[2,64,1280]{2,0,1:T(2,128)(2,1)}), bf16[2,64,1280]{2,0,1:T(2,128)(2,1)}, u32[]{:S(2)}, u32[]{:S(2)}) async-start(bf16[2,64,1280]{2,0,1:T(2,128)(2,1)} %copy.350), calls=%async_computation.16 | async-start | bytes 655360 | tf_op jit(solution)/shard_map/all_to_all | solution.py:122
  408.8 19.5 %all-to-all-start.17 = ((bf16[2,64,1280]{2,0,1:T(2,128)(2,1)}), bf16[2,64,1280]{2,0,1:T(2,128)(2,1)}, u32[]{:S(2)}, u32[]{:S(2)}) async-start(bf16[2,64,1280]{2,0,1:T(2,128)(2,1)} %collective-permute-done.17), calls=%async_computation.17 | async-start | bytes 655360 | tf_op jit(solution)/shard_map/all_to_all | solution.py:124
  434.1 19.5 %all-to-all-start.18 = ((bf16[2,64,1280]{2,0,1:T(2,128)(2,1)}), bf16[2,64,1280]{2,0,1:T(2,128)(2,1)}, u32[]{:S(2)}, u32[]{:S(2)}) async-start(bf16[2,64,1280]{2,0,1:T(2,128)(2,1)} %copy.352), calls=%async_computation.18 | async-start | bytes 655360 | tf_op jit(solution)/shard_map/all_to_all | solution.py:122
  453.6 19.5 %all-to-all-start.19 = ((bf16[2,64,1280]{2,0,1:T(2,128)(2,1)}), bf16[2,64,1280]{2,0,1:T(2,128)(2,1)}, u32[]{:S(2)}, u32[]{:S(2)}) async-start(bf16[2,64,1280]{2,0,1:T(2,128)(2,1)} %collective-permute-done.19), calls=%async_computation.19 | async-start | bytes 655360 | tf_op jit(solution)/shard_map/all_to_all | solution.py:124
  478.9 19.5 %all-to-all-start.20 = ((bf16[2,64,1280]{2,0,1:T(2,128)(2,1)}), bf16[2,64,1280]{2,0,1:T(2,128)(2,1)}, u32[]{:S(2)}, u32[]{:S(2)}) async-start(bf16[2,64,1280]{2,0,1:T(2,128)(2,1)} %copy.354), calls=%async_computation.20 | async-start | bytes 655360 | tf_op jit(solution)/shard_map/all_to_all | solution.py:122
  498.4 19.5 %all-to-all-start.21 = ((bf16[2,64,1280]{2,0,1:T(2,128)(2,1)}), bf16[2,64,1280]{2,0,1:T(2,128)(2,1)}, u32[]{:S(2)}, u32[]{:S(2)}) async-start(bf16[2,64,1280]{2,0,1:T(2,128)(2,1)} %collective-permute-done.21), calls=%async_computation.21 | async-start | bytes 655360 | tf_op jit(solution)/shard_map/all_to_all | solution.py:124
  523.7 19.5 %all-to-all-start.22 = ((bf16[2,64,1280]{2,0,1:T(2,128)(2,1)}), bf16[2,64,1280]{2,0,1:T(2,128)(2,1)}, u32[]{:S(2)}, u32[]{:S(2)}) async-start(bf16[2,64,1280]{2,0,1:T(2,128)(2,1)} %copy.356), calls=%async_computation.22 | async-start | bytes 655360 | tf_op jit(solution)/shard_map/all_to_all | solution.py:122
  543.2 19.5 %all-to-all-start.23 = ((bf16[2,64,1280]{2,0,1:T(2,128)(2,1)}), bf16[2,64,1280]{2,0,1:T(2,128)(2,1)}, u32[]{:S(2)}, u32[]{:S(2)}) async-start(bf16[2,64,1280]{2,0,1:T(2,128)(2,1)} %collective-permute-done.23), calls=%async_computation.23 | async-start | bytes 655360 | tf_op jit(solution)/shard_map/all_to_all | solution.py:124
  568.4 19.5 %all-to-all-start.24 = ((bf16[2,64,1280]{2,0,1:T(2,128)(2,1)}), bf16[2,64,1280]{2,0,1:T(2,128)(2,1)}, u32[]{:S(2)}, u32[]{:S(2)}) async-start(bf16[2,64,1280]{2,0,1:T(2,128)(2,1)} %copy.358), calls=%async_computation.24 | async-start | bytes 655360 | tf_op jit(solution)/shard_map/all_to_all | solution.py:122
  587.9 19.5 %all-to-all-start.25 = ((bf16[2,64,1280]{2,0,1:T(2,128)(2,1)}), bf16[2,64,1280]{2,0,1:T(2,128)(2,1)}, u32[]{:S(2)}, u32[]{:S(2)}) async-start(bf16[2,64,1280]{2,0,1:T(2,128)(2,1)} %collective-permute-done.25), calls=%async_computation.25 | async-start | bytes 655360 | tf_op jit(solution)/shard_map/all_to_all | solution.py:124
  613.2 98.2 %all-to-all-start.26 = ((bf16[2,64,1280]{2,0,1:T(2,128)(2,1)}), bf16[2,64,1280]{2,0,1:T(2,128)(2,1)}, u32[]{:S(2)}, u32[]{:S(2)}) async-start(bf16[2,64,1280]{2,0,1:T(2,128)(2,1)} %copy.360), calls=%async_computation.26 | async-start | bytes 655360 | tf_op jit(solution)/shard_map/all_to_all | solution.py:122
  624.4 87.0 %collective-permute-start.27 = (bf16[2,64,1280]{2,0,1:T(2,128)(2,1)S(1)}, bf16[2,64,1280]{2,0,1:T(2,128)(2,1)}, u32[]{:S(2)}, u32[]{:S(2)}) collective-permute-start(bf16[2,64,1280]{2,0,1:T(2,128)(2,1)S(1)} %copy.361), channel_id=1, source_target_pairs={{64,0},{65,1},{66,2},{67,3},{68,4},{69,5},{70,6},{71,7},{72,8},{73... | collective-permute-start | bytes 983048 | tf_op jit(solution)/shard_map/ppermute | solution.py:121
  711.4 23.3 %all-to-all-start.27 = ((bf16[2,64,1280]{2,0,1:T(2,128)(2,1)}), bf16[2,64,1280]{2,0,1:T(2,128)(2,1)}, u32[]{:S(2)}, u32[]{:S(2)}) async-start(bf16[2,64,1280]{2,0,1:T(2,128)(2,1)} %collective-permute-done.27), calls=%async_computation.27 | async-start | bytes 655360 | tf_op jit(solution)/shard_map/all_to_all | solution.py:124
  (129 other events, 1603.5 us)

commit v6 on v4

--- a/solution.py
+++ b/solution.py
@@ -65,15 +65,9 @@
         destinations[:, :, None, :] == jnp.arange(peer_count, dtype=jnp.int32)[None, None, :, None]
     ).astype(jnp.bfloat16)
 
-    x = inputs.reshape(micro_count, batch_rows, feature_count)
-    keep_x = jnp.zeros((row_count, feature_count), jnp.bfloat16)
-    keep_inv = jnp.zeros((row_count, 1), jnp.float32)
-    keep_normed = jnp.zeros((row_count, feature_count), jnp.bfloat16)
-    keep_active = jnp.zeros((row_count, down_proj.shape[0]), jnp.bfloat16)
-    keep_slope = jnp.zeros((row_count, down_proj.shape[0]), jnp.float32)
-    upstream = None
-    for k in range(sections):
-        flat = x.reshape(row_count, feature_count)
+    units = down_proj.shape[0]
+
+    def forward_layer(flat):
         x_float, inv_rms, normed = normalize(flat, gain_row)
         hidden = contract_last(normed, down_proj)
         gelu_value, gelu_slope = gelu_parts(hidden)
@@ -81,25 +75,48 @@
         outputs = (x_float + jnp.dot(active, up_proj, preferred_element_type=jnp.float32)).astype(
             jnp.bfloat16
         )
+        return (inv_rms, normed, active, gelu_slope, outputs)
+
+    forward_pairs = [(j, j + 1) for j in range(sections - 1)]
+
+    def forward_step(k, carry):
+        flat, keep_x, keep_inv, keep_normed, keep_active, keep_slope = carry
+        inv_rms, normed, active, gelu_slope, outputs = forward_layer(flat)
         mine = section_now == k
         keep_x = jnp.where(mine, flat, keep_x)
         keep_inv = jnp.where(mine, inv_rms, keep_inv)
         keep_normed = jnp.where(mine, normed, keep_normed)
         keep_active = jnp.where(mine, active, keep_active)
         keep_slope = jnp.where(mine, gelu_slope, keep_slope)
-        if k < sections - 1:
-            packed = permute_rows(
-                send_onehot[k], outputs.reshape(micro_count, batch_rows, feature_count), "mdq,mqf->mdf"
-            )
-            received = lax.all_to_all(packed, "peer", 1, 1, tiled=True)
-            x = lax.ppermute(received, "section", [(k, k + 1)])
-        else:
-            upstream = outputs
+        packed = permute_rows(
+            send_onehot[k], outputs.reshape(micro_count, batch_rows, feature_count), "mdq,mqf->mdf"
+        )
+        received = lax.all_to_all(packed, "peer", 1, 1, tiled=True)
+        moved = lax.ppermute(received, "section", forward_pairs)
+        return (moved.reshape(row_count, feature_count), keep_x, keep_inv, keep_normed, keep_active, keep_slope)
+
+    carry = (
+        inputs,
+        jnp.zeros((row_count, feature_count), jnp.bfloat16),
+        jnp.zeros((row_count, 1), jnp.float32),
+        jnp.zeros((row_count, feature_count), jnp.bfloat16),
+        jnp.zeros((row_count, units), jnp.bfloat16),
+        jnp.zeros((row_count, units), jnp.float32),
+    )
+    flat, keep_x, keep_inv, keep_normed, keep_active, keep_slope = lax.fori_loop(
+        0, sections - 1, forward_step, carry
+    )
+    inv_rms, normed, active, gelu_slope, upstream = forward_layer(flat)
+    mine = section_now == sections - 1
+    keep_x = jnp.where(mine, flat, keep_x)
+    keep_inv = jnp.where(mine, inv_rms, keep_inv)
+    keep_normed = jnp.where(mine, normed, keep_normed)
+    keep_active = jnp.where(mine, active, keep_active)
+    keep_slope = jnp.where(mine, gelu_slope, keep_slope)
 
     x_float = keep_x.astype(jnp.float32)
-    keep_upstream = jnp.zeros((row_count, feature_count), jnp.bfloat16)
-    keep_grad_hidden = jnp.zeros((row_count, down_proj.shape[0]), jnp.bfloat16)
-    for k in reversed(range(sections)):
+
+    def backward_layer(upstream):
         grad_active = contract_last(upstream, up_proj)
         grad_hidden = (grad_active * keep_slope).astype(jnp.bfloat16)
         grad_normed = jnp.dot(grad_hidden, down_proj, preferred_element_type=jnp.float32) * gain_float
@@ -108,17 +125,36 @@
             upstream.astype(jnp.float32)
             + keep_inv * (grad_normed - x_float * keep_inv * keep_inv * inner_term)
         ).astype(jnp.bfloat16)
+        return (grad_hidden, grad_rows)
+
+    backward_pairs = [(j + 1, j) for j in range(sections - 1)]
+
+    def backward_step(t, carry):
+        upstream, keep_upstream, keep_grad_hidden = carry
+        k = sections - 1 - t
+        grad_hidden, grad_rows = backward_layer(upstream)
         mine = section_now == k
         keep_upstream = jnp.where(mine, upstream, keep_upstream)
         keep_grad_hidden = jnp.where(mine, grad_hidden, keep_grad_hidden)
-        if k > 0:
-            sent = lax.all_to_all(
-                grad_rows.reshape(micro_count, batch_rows, feature_count), "peer", 1, 1, tiled=True
-            )
-            moved = lax.ppermute(sent, "section", [(k, k - 1)])
-            upstream = permute_rows(send_onehot[k - 1], moved, "mdq,mdf->mqf").reshape(
-                row_count, feature_count
-            )
+        sent = lax.all_to_all(
+            grad_rows.reshape(micro_count, batch_rows, feature_count), "peer", 1, 1, tiled=True
+        )
+        moved = lax.ppermute(sent, "section", backward_pairs)
+        upstream = permute_rows(send_onehot[k - 1], moved, "mdq,mdf->mqf").reshape(
+            row_count, feature_count
+        )
+        return (upstream, keep_upstream, keep_grad_hidden)
+
+    carry = (
+        upstream,
+        jnp.zeros((row_count, feature_count), jnp.bfloat16),
+        jnp.zeros((row_count, units), jnp.bfloat16),
+    )
+    upstream, keep_upstream, keep_grad_hidden = lax.fori_loop(0, sections - 1, backward_step, carry)
+    grad_hidden, grad_rows = backward_layer(upstream)
+    mine = section_now == 0
+    keep_upstream = jnp.where(mine, upstream, keep_upstream)
+    keep_grad_hidden = jnp.where(mine, grad_hidden, keep_grad_hidden)
 
     bits_count = peer_count.bit_length() - 1
     peers = jnp.arange(peer_count, dtype=jnp.int32)

time: 752 us -> 812 us (1.080)
  blocking collectives: 346 us -> 0 us
  waiting for transfers between devices: 274 us -> 520 us
  starting transfers between devices: 37.8 us -> 154 us
  matrix products: 29.1 us -> 54.2 us
  other arithmetic: 22.9 us -> 37.9 us
    all_to_all x13 -> x0, blocking collectives: 346 us -> none  [the longest x7 189 us: local(): received = lax.all_to_all(packed, 'peer', 1, 1, tiled=True)]
    all_to_all x1 -> x14, waiting for transfers between devices: 16.6 us -> 252 us  [the longest x7 135 us: backward_step(): lax.all_to_all(grad_rows.reshape(micro_count, batch_rows, feature_count),...]
    all_to_all x1 -> x14, starting transfers between devices: 7.23 us -> 95.1 us  [the longest x7 50.8 us: forward_step(): received = lax.all_to_all(packed, 'peer', 1, 1, tiled=True)]
    ppermute x14, starting transfers between devices: 14.5 us -> 43.1 us  [the longest x7 33.2 us: forward_step(): moved = lax.ppermute(received, 'section', forward_pairs)]
    select_n x0 -> x28, other arithmetic: none -> 24 us  [the longest x7 10.3 us: forward_step(): keep_slope = jnp.where(mine, gelu_slope, keep_slope)]
    dot_general x16, matrix products: 9.3 us -> 31.8 us  [contract_last(): lax.dot_general(left, right, (((1,), (1,)), ((), ())), preferred_element_...]
    ppermute x14, waiting for transfers between devices: 223 us -> 234 us  [the longest x7 134 us: backward_step(): moved = lax.ppermute(sent, 'section', backward_pairs)]
  transfers between devices with their start and end apart: 21 -> 34, of which waited for: 9 -> 34; matrix products, arithmetic and copies ran while one was open for 1% -> 3% of each run, Pallas kernels for 0% -> 0%
where the time goes in v6:
time: 812 us; the launch traced here: 804 us
  waiting for transfers between devices  520 us (64%)
  starting transfers between devices  154 us (19%)
  matrix products  54.2 us (7%)
  other arithmetic  37.9 us (5%)
  local copies, waits for them, and re-layouts  35.3 us (4%)
    all_to_all x7, waiting for transfers between devices, backward_step(): lax.all_to_all(grad_rows.reshape(micro_count, batch_rows, feature_count),...  135 us
    ppermute x7, waiting for transfers between devices, backward_step(): moved = lax.ppermute(sent, 'section', backward_pairs)  134 us
    all_to_all x7, waiting for transfers between devices, forward_step(): received = lax.all_to_all(packed, 'peer', 1, 1, tiled=True)  117 us
    ppermute x7, waiting for transfers between devices, forward_step(): moved = lax.ppermute(received, 'section', forward_pairs)  100 us
    all_to_all x7, starting transfers between devices, forward_step(): received = lax.all_to_all(packed, 'peer', 1, 1, tiled=True)  50.8 us
    all_to_all x7, starting transfers between devices, backward_step(): lax.all_to_all(grad_rows.reshape(micro_count, batch_rows, feature_count),...  44.3 us
    ppermute x6, waiting for transfers between devices, local(): arrived = lax.ppermute(outgoing.astype(jnp.bfloat16), 'peer', pairs)  33.8 us
    ppermute x7, starting transfers between devices, forward_step(): moved = lax.ppermute(received, 'section', forward_pairs)  33.2 us
  transfers between devices with their start and end apart: 34, of which 34 were waited for; matrix products, arithmetic and copies ran while one was open for 3% of the time, Pallas kernels for 0%

profile of v6, /device:TPU:6, one launch (start us, length us, event | category | flops | bytes accessed | tf_op | source)
XLA Modules:
  0.0 804.0 jit_solution(14623314952134285208)
XLA Ops:
  5.2 367.9 %while.48 = (s32[]{:T(128)}, bf16[128,2560]{1,0:T(8,128)(2,1)S(1)}, bf16[128,2560]{1,0:T(8,128)(2,1)S(1)}, f32[128,1]{0,1:T(1,128)}, bf16[128,2560]{1,0:T(8,128)...) while((s32[]{:T(128)}, bf16[128,2560]{1,0:T(8,128)(2,1)S(1)}, ...), condition=%wide.region_3.4_spmd.clone, body=%wide.region_1.3_spmd.clone.sunk | while | flops 300788864 | bytes 23730148 | solution.py:106
  27.2 17.4 %all-to-all-done = bf16[2,64,2560]{2,0,1:T(2,128)(2,1)S(1)} async-done(((bf16[2,64,2560]{2,0,1:T(2,128)(2,1)}), bf16[2,64,2560]{2,0,1:T(2,128)(2,1)S(1)}, u32[]{:S(2)}, u32[]{:S(2)}) %all-to-all-start) | async-done | bytes 655392 | tf_op jit(solution)/shard_map/while/body/eval_jaxpr/all_to_all | solution.py:94
  49.0 14.3 %collective-permute-done = bf16[2,64,2560]{2,1,0:T(8,128)(2,1)S(1)} collective-permute-done((bf16[2,64,2560]{2,1,0:T(8,128)(2,1)S(1)}, bf16[2,64,2560]{2,1,0:T(8,128)(2,1)S(1)}, u32[]{:S(2)}, u32[]{:S(2)}) %collective-permute-start) | collective-permute-done | bytes 655392 | tf_op jit(solution)/shard_map/while/body/eval_jaxpr/ppermute | solution.py:95
  78.5 16.5 %all-to-all-done = bf16[2,64,2560]{2,0,1:T(2,128)(2,1)S(1)} async-done(((bf16[2,64,2560]{2,0,1:T(2,128)(2,1)}), bf16[2,64,2560]{2,0,1:T(2,128)(2,1)S(1)}, u32[]{:S(2)}, u32[]{:S(2)}) %all-to-all-start) | async-done | bytes 655392 | tf_op jit(solution)/shard_map/while/body/eval_jaxpr/all_to_all | solution.py:94
  129.7 16.5 %all-to-all-done = bf16[2,64,2560]{2,0,1:T(2,128)(2,1)S(1)} async-done(((bf16[2,64,2560]{2,0,1:T(2,128)(2,1)}), bf16[2,64,2560]{2,0,1:T(2,128)(2,1)S(1)}, u32[]{:S(2)}, u32[]{:S(2)}) %all-to-all-start) | async-done | bytes 655392 | tf_op jit(solution)/shard_map/while/body/eval_jaxpr/all_to_all | solution.py:94
  181.0 16.5 %all-to-all-done = bf16[2,64,2560]{2,0,1:T(2,128)(2,1)S(1)} async-done(((bf16[2,64,2560]{2,0,1:T(2,128)(2,1)}), bf16[2,64,2560]{2,0,1:T(2,128)(2,1)S(1)}, u32[]{:S(2)}, u32[]{:S(2)}) %all-to-all-start) | async-done | bytes 655392 | tf_op jit(solution)/shard_map/while/body/eval_jaxpr/all_to_all | solution.py:94
  232.2 16.5 %all-to-all-done = bf16[2,64,2560]{2,0,1:T(2,128)(2,1)S(1)} async-done(((bf16[2,64,2560]{2,0,1:T(2,128)(2,1)}), bf16[2,64,2560]{2,0,1:T(2,128)(2,1)S(1)}, u32[]{:S(2)}, u32[]{:S(2)}) %all-to-all-start) | async-done | bytes 655392 | tf_op jit(solution)/shard_map/while/body/eval_jaxpr/all_to_all | solution.py:94
  283.5 16.5 %all-to-all-done = bf16[2,64,2560]{2,0,1:T(2,128)(2,1)S(1)} async-done(((bf16[2,64,2560]{2,0,1:T(2,128)(2,1)}), bf16[2,64,2560]{2,0,1:T(2,128)(2,1)S(1)}, u32[]{:S(2)}, u32[]{:S(2)}) %all-to-all-start) | async-done | bytes 655392 | tf_op jit(solution)/shard_map/while/body/eval_jaxpr/all_to_all | solution.py:94
  335.7 16.5 %all-to-all-done = bf16[2,64,2560]{2,0,1:T(2,128)(2,1)S(1)} async-done(((bf16[2,64,2560]{2,0,1:T(2,128)(2,1)}), bf16[2,64,2560]{2,0,1:T(2,128)(2,1)S(1)}, u32[]{:S(2)}, u32[]{:S(2)}) %all-to-all-start) | async-done | bytes 655392 | tf_op jit(solution)/shard_map/while/body/eval_jaxpr/all_to_all | solution.py:94
  378.9 363.0 %while.49 = (s32[]{:T(128)}, bf16[128,2560]{1,0:T(8,128)(2,1)S(1)}, bf16[128,2560]{1,0:T(8,128)(2,1)}, bf16[128,192]{0,1:T(8,128)(2,1)S(1)}, bf16[7,2,64,64]{2,3...) while((s32[]{:T(128)}, bf16[128,2560]{1,0:T(8,128)(2,1)S(1)}, ...), condition=%wide.region_7.8_spmd.clone, body=%wide.region_5.7_spmd.clone.sunk | while | flops 298287104 | bytes 29176716 | solution.py:153
  389.2 19.3 %all-to-all-done.1 = bf16[2,64,2560]{2,0,1:T(2,128)(2,1)S(1)} async-done(((bf16[2,64,2560]{2,0,1:T(2,128)(2,1)}), bf16[2,64,2560]{2,0,1:T(2,128)(2,1)S(1)}, u32[]{:S(2)}, u32[]{:S(2)}) %all-to-all-start.1) | async-done | bytes 655392 | tf_op jit(solution)/shard_map/while/body/eval_jaxpr/all_to_all | solution.py:139
  410.2 19.5 %collective-permute-done.1 = bf16[2,64,2560]{2,1,0:T(8,128)(2,1)S(1)} collective-permute-done((bf16[2,64,2560]{2,1,0:T(8,128)(2,1)S(1)}, bf16[2,64,2560]{2,1,0:T(8,128)(2,1)S(1)}, u32[]{:S(2)}, u32[]{:S(2)}) %collective-permute-start.1) | collective-permute-done | bytes 655392 | tf_op jit(solution)/shard_map/while/body/eval_jaxpr/ppermute | solution.py:142
  441.4 19.3 %all-to-all-done.1 = bf16[2,64,2560]{2,0,1:T(2,128)(2,1)S(1)} async-done(((bf16[2,64,2560]{2,0,1:T(2,128)(2,1)}), bf16[2,64,2560]{2,0,1:T(2,128)(2,1)S(1)}, u32[]{:S(2)}, u32[]{:S(2)}) %all-to-all-start.1) | async-done | bytes 655392 | tf_op jit(solution)/shard_map/while/body/eval_jaxpr/all_to_all | solution.py:139
  462.5 19.5 %collective-permute-done.1 = bf16[2,64,2560]{2,1,0:T(8,128)(2,1)S(1)} collective-permute-done((bf16[2,64,2560]{2,1,0:T(8,128)(2,1)S(1)}, bf16[2,64,2560]{2,1,0:T(8,128)(2,1)S(1)}, u32[]{:S(2)}, u32[]{:S(2)}) %collective-permute-start.1) | collective-permute-done | bytes 655392 | tf_op jit(solution)/shard_map/while/body/eval_jaxpr/ppermute | solution.py:142
  493.6 19.3 %all-to-all-done.1 = bf16[2,64,2560]{2,0,1:T(2,128)(2,1)S(1)} async-done(((bf16[2,64,2560]{2,0,1:T(2,128)(2,1)}), bf16[2,64,2560]{2,0,1:T(2,128)(2,1)S(1)}, u32[]{:S(2)}, u32[]{:S(2)}) %all-to-all-start.1) | async-done | bytes 655392 | tf_op jit(solution)/shard_map/while/body/eval_jaxpr/all_to_all | solution.py:139
  514.7 19.5 %collective-permute-done.1 = bf16[2,64,2560]{2,1,0:T(8,128)(2,1)S(1)} collective-permute-done((bf16[2,64,2560]{2,1,0:T(8,128)(2,1)S(1)}, bf16[2,64,2560]{2,1,0:T(8,128)(2,1)S(1)}, u32[]{:S(2)}, u32[]{:S(2)}) %collective-permute-start.1) | collective-permute-done | bytes 655392 | tf_op jit(solution)/shard_map/while/body/eval_jaxpr/ppermute | solution.py:142
  545.8 19.3 %all-to-all-done.1 = bf16[2,64,2560]{2,0,1:T(2,128)(2,1)S(1)} async-done(((bf16[2,64,2560]{2,0,1:T(2,128)(2,1)}), bf16[2,64,2560]{2,0,1:T(2,128)(2,1)S(1)}, u32[]{:S(2)}, u32[]{:S(2)}) %all-to-all-start.1) | async-done | bytes 655392 | tf_op jit(solution)/shard_map/while/body/eval_jaxpr/all_to_all | solution.py:139
  566.9 19.5 %collective-permute-done.1 = bf16[2,64,2560]{2,1,0:T(8,128)(2,1)S(1)} collective-permute-done((bf16[2,64,2560]{2,1,0:T(8,128)(2,1)S(1)}, bf16[2,64,2560]{2,1,0:T(8,128)(2,1)S(1)}, u32[]{:S(2)}, u32[]{:S(2)}) %collective-permute-start.1) | collective-permute-done | bytes 655392 | tf_op jit(solution)/shard_map/while/body/eval_jaxpr/ppermute | solution.py:142
  598.0 19.3 %all-to-all-done.1 = bf16[2,64,2560]{2,0,1:T(2,128)(2,1)S(1)} async-done(((bf16[2,64,2560]{2,0,1:T(2,128)(2,1)}), bf16[2,64,2560]{2,0,1:T(2,128)(2,1)S(1)}, u32[]{:S(2)}, u32[]{:S(2)}) %all-to-all-start.1) | async-done | bytes 655392 | tf_op jit(solution)/shard_map/while/body/eval_jaxpr/all_to_all | solution.py:139
  619.1 18.7 %collective-permute-done.1 = bf16[2,64,2560]{2,1,0:T(8,128)(2,1)S(1)} collective-permute-done((bf16[2,64,2560]{2,1,0:T(8,128)(2,1)S(1)}, bf16[2,64,2560]{2,1,0:T(8,128)(2,1)S(1)}, u32[]{:S(2)}, u32[]{:S(2)}) %collective-permute-start.1) | collective-permute-done | bytes 655392 | tf_op jit(solution)/shard_map/while/body/eval_jaxpr/ppermute | solution.py:142
  649.5 19.3 %all-to-all-done.1 = bf16[2,64,2560]{2,0,1:T(2,128)(2,1)S(1)} async-done(((bf16[2,64,2560]{2,0,1:T(2,128)(2,1)}), bf16[2,64,2560]{2,0,1:T(2,128)(2,1)S(1)}, u32[]{:S(2)}, u32[]{:S(2)}) %all-to-all-start.1) | async-done | bytes 655392 | tf_op jit(solution)/shard_map/while/body/eval_jaxpr/all_to_all | solution.py:139
  670.5 18.8 %collective-permute-done.1 = bf16[2,64,2560]{2,1,0:T(8,128)(2,1)S(1)} collective-permute-done((bf16[2,64,2560]{2,1,0:T(8,128)(2,1)S(1)}, bf16[2,64,2560]{2,1,0:T(8,128)(2,1)S(1)}, u32[]{:S(2)}, u32[]{:S(2)}) %collective-permute-start.1) | collective-permute-done | bytes 655392 | tf_op jit(solution)/shard_map/while/body/eval_jaxpr/ppermute | solution.py:142
  700.9 19.3 %all-to-all-done.1 = bf16[2,64,2560]{2,0,1:T(2,128)(2,1)S(1)} async-done(((bf16[2,64,2560]{2,0,1:T(2,128)(2,1)}), bf16[2,64,2560]{2,0,1:T(2,128)(2,1)S(1)}, u32[]{:S(2)}, u32[]{:S(2)}) %all-to-all-start.1) | async-done | bytes 655392 | tf_op jit(solution)/shard_map/while/body/eval_jaxpr/all_to_all | solution.py:139
  722.0 18.8 %collective-permute-done.1 = bf16[2,64,2560]{2,1,0:T(8,128)(2,1)S(1)} collective-permute-done((bf16[2,64,2560]{2,1,0:T(8,128)(2,1)S(1)}, bf16[2,64,2560]{2,1,0:T(8,128)(2,1)S(1)}, u32[]{:S(2)}, u32[]{:S(2)}) %collective-permute-start.1) | collective-permute-done | bytes 655392 | tf_op jit(solution)/shard_map/while/body/eval_jaxpr/ppermute | solution.py:142
  (447 shorter events, 401.3 us)
Async XLA Ops:
  11.3 33.3 %all-to-all-start = ((bf16[2,64,2560]{2,0,1:T(2,128)(2,1)}), bf16[2,64,2560]{2,0,1:T(2,128)(2,1)S(1)}, u32[]{:S(2)}, u32[]{:S(2)}) async-start(bf16[2,64,2560]{2,0,1:T(2,128)(2,1)} %copy.46), calls=%async_computation | async-start | bytes 1310720 | tf_op jit(solution)/shard_map/while/body/eval_jaxpr/all_to_all | solution.py:94
  69.6 25.4 %all-to-all-start = ((bf16[2,64,2560]{2,0,1:T(2,128)(2,1)}), bf16[2,64,2560]{2,0,1:T(2,128)(2,1)S(1)}, u32[]{:S(2)}, u32[]{:S(2)}) async-start(bf16[2,64,2560]{2,0,1:T(2,128)(2,1)} %copy.46), calls=%async_computation | async-start | bytes 1310720 | tf_op jit(solution)/shard_map/while/body/eval_jaxpr/all_to_all | solution.py:94
  120.8 25.4 %all-to-all-start = ((bf16[2,64,2560]{2,0,1:T(2,128)(2,1)}), bf16[2,64,2560]{2,0,1:T(2,128)(2,1)S(1)}, u32[]{:S(2)}, u32[]{:S(2)}) async-start(bf16[2,64,2560]{2,0,1:T(2,128)(2,1)} %copy.46), calls=%async_computation | async-start | bytes 1310720 | tf_op jit(solution)/shard_map/while/body/eval_jaxpr/all_to_all | solution.py:94
  172.1 25.5 %all-to-all-start = ((bf16[2,64,2560]{2,0,1:T(2,128)(2,1)}), bf16[2,64,2560]{2,0,1:T(2,128)(2,1)S(1)}, u32[]{:S(2)}, u32[]{:S(2)}) async-start(bf16[2,64,2560]{2,0,1:T(2,128)(2,1)} %copy.46), calls=%async_computation | async-start | bytes 1310720 | tf_op jit(solution)/shard_map/while/body/eval_jaxpr/all_to_all | solution.py:94
  197.6 19.5 %collective-permute-start = (bf16[2,64,2560]{2,1,0:T(8,128)(2,1)S(1)}, bf16[2,64,2560]{2,1,0:T(8,128)(2,1)S(1)}, u32[]{:S(2)}, u32[]{:S(2)}) collective-permute-start(bf16[2,64,2560]{2,1,0:T(8,128)(2,1)S(1)} %copy.47), channel_id=1, source_target_pairs={{0,64},{64,128},{128,192},{192,256},{256,320},{320,384},{384,448},... | collective-permute-start | bytes 1966088 | tf_op jit(solution)/shard_map/while/body/eval_jaxpr/ppermute | solution.py:95
  223.3 25.4 %all-to-all-start = ((bf16[2,64,2560]{2,0,1:T(2,128)(2,1)}), bf16[2,64,2560]{2,0,1:T(2,128)(2,1)S(1)}, u32[]{:S(2)}, u32[]{:S(2)}) async-start(bf16[2,64,2560]{2,0,1:T(2,128)(2,1)} %copy.46), calls=%async_computation | async-start | bytes 1310720 | tf_op jit(solution)/shard_map/while/body/eval_jaxpr/all_to_all | solution.py:94
  274.6 25.5 %all-to-all-start = ((bf16[2,64,2560]{2,0,1:T(2,128)(2,1)}), bf16[2,64,2560]{2,0,1:T(2,128)(2,1)S(1)}, u32[]{:S(2)}, u32[]{:S(2)}) async-start(bf16[2,64,2560]{2,0,1:T(2,128)(2,1)} %copy.46), calls=%async_computation | async-start | bytes 1310720 | tf_op jit(solution)/shard_map/while/body/eval_jaxpr/all_to_all | solution.py:94
  300.1 20.4 %collective-permute-start = (bf16[2,64,2560]{2,1,0:T(8,128)(2,1)S(1)}, bf16[2,64,2560]{2,1,0:T(8,128)(2,1)S(1)}, u32[]{:S(2)}, u32[]{:S(2)}) collective-permute-start(bf16[2,64,2560]{2,1,0:T(8,128)(2,1)S(1)} %copy.47), channel_id=1, source_target_pairs={{0,64},{64,128},{128,192},{192,256},{256,320},{320,384},{384,448},... | collective-permute-start | bytes 1966088 | tf_op jit(solution)/shard_map/while/body/eval_jaxpr/ppermute | solution.py:95
  326.8 25.4 %all-to-all-start = ((bf16[2,64,2560]{2,0,1:T(2,128)(2,1)}), bf16[2,64,2560]{2,0,1:T(2,128)(2,1)S(1)}, u32[]{:S(2)}, u32[]{:S(2)}) async-start(bf16[2,64,2560]{2,0,1:T(2,128)(2,1)} %copy.46), calls=%async_computation | async-start | bytes 1310720 | tf_op jit(solution)/shard_map/while/body/eval_jaxpr/all_to_all | solution.py:94
  352.3 20.7 %collective-permute-start = (bf16[2,64,2560]{2,1,0:T(8,128)(2,1)S(1)}, bf16[2,64,2560]{2,1,0:T(8,128)(2,1)S(1)}, u32[]{:S(2)}, u32[]{:S(2)}) collective-permute-start(bf16[2,64,2560]{2,1,0:T(8,128)(2,1)S(1)} %copy.47), channel_id=1, source_target_pairs={{0,64},{64,128},{128,192},{192,256},{256,320},{320,384},{384,448},... | collective-permute-start | bytes 1966088 | tf_op jit(solution)/shard_map/while/body/eval_jaxpr/ppermute | solution.py:95
  383.0 25.4 %all-to-all-start.1 = ((bf16[2,64,2560]{2,0,1:T(2,128)(2,1)}), bf16[2,64,2560]{2,0,1:T(2,128)(2,1)S(1)}, u32[]{:S(2)}, u32[]{:S(2)}) async-start(bf16[2,64,2560]{2,0,1:T(2,128)(2,1)} %copy.48), calls=%async_computation.1 | async-start | bytes 1310720 | tf_op jit(solution)/shard_map/while/body/eval_jaxpr/all_to_all | solution.py:139
  408.5 21.2 %collective-permute-start.1 = (bf16[2,64,2560]{2,1,0:T(8,128)(2,1)S(1)}, bf16[2,64,2560]{2,1,0:T(8,128)(2,1)S(1)}, u32[]{:S(2)}, u32[]{:S(2)}) collective-permute-start(bf16[2,64,2560]{2,1,0:T(8,128)(2,1)S(1)} %copy.49), channel_id=1, source_target_pairs={{64,0},{128,64},{192,128},{256,192},{320,256},{384,320},{448,384},... | collective-permute-start | bytes 1966088 | tf_op jit(solution)/shard_map/while/body/eval_jaxpr/ppermute | solution.py:142
  435.0 25.7 %all-to-all-start.1 = ((bf16[2,64,2560]{2,0,1:T(2,128)(2,1)}), bf16[2,64,2560]{2,0,1:T(2,128)(2,1)S(1)}, u32[]{:S(2)}, u32[]{:S(2)}) async-start(bf16[2,64,2560]{2,0,1:T(2,128)(2,1)} %copy.48), calls=%async_computation.1 | async-start | bytes 1310720 | tf_op jit(solution)/shard_map/while/body/eval_jaxpr/all_to_all | solution.py:139
  460.7 21.2 %collective-permute-start.1 = (bf16[2,64,2560]{2,1,0:T(8,128)(2,1)S(1)}, bf16[2,64,2560]{2,1,0:T(8,128)(2,1)S(1)}, u32[]{:S(2)}, u32[]{:S(2)}) collective-permute-start(bf16[2,64,2560]{2,1,0:T(8,128)(2,1)S(1)} %copy.49), channel_id=1, source_target_pairs={{64,0},{128,64},{192,128},{256,192},{320,256},{384,320},{448,384},... | collective-permute-start | bytes 1966088 | tf_op jit(solution)/shard_map/while/body/eval_jaxpr/ppermute | solution.py:142
  487.2 25.6 %all-to-all-start.1 = ((bf16[2,64,2560]{2,0,1:T(2,128)(2,1)}), bf16[2,64,2560]{2,0,1:T(2,128)(2,1)S(1)}, u32[]{:S(2)}, u32[]{:S(2)}) async-start(bf16[2,64,2560]{2,0,1:T(2,128)(2,1)} %copy.48), calls=%async_computation.1 | async-start | bytes 1310720 | tf_op jit(solution)/shard_map/while/body/eval_jaxpr/all_to_all | solution.py:139
  512.9 21.2 %collective-permute-start.1 = (bf16[2,64,2560]{2,1,0:T(8,128)(2,1)S(1)}, bf16[2,64,2560]{2,1,0:T(8,128)(2,1)S(1)}, u32[]{:S(2)}, u32[]{:S(2)}) collective-permute-start(bf16[2,64,2560]{2,1,0:T(8,128)(2,1)S(1)} %copy.49), channel_id=1, source_target_pairs={{64,0},{128,64},{192,128},{256,192},{320,256},{384,320},{448,384},... | collective-permute-start | bytes 1966088 | tf_op jit(solution)/shard_map/while/body/eval_jaxpr/ppermute | solution.py:142
  539.4 25.7 %all-to-all-start.1 = ((bf16[2,64,2560]{2,0,1:T(2,128)(2,1)}), bf16[2,64,2560]{2,0,1:T(2,128)(2,1)S(1)}, u32[]{:S(2)}, u32[]{:S(2)}) async-start(bf16[2,64,2560]{2,0,1:T(2,128)(2,1)} %copy.48), calls=%async_computation.1 | async-start | bytes 1310720 | tf_op jit(solution)/shard_map/while/body/eval_jaxpr/all_to_all | solution.py:139
  565.2 21.2 %collective-permute-start.1 = (bf16[2,64,2560]{2,1,0:T(8,128)(2,1)S(1)}, bf16[2,64,2560]{2,1,0:T(8,128)(2,1)S(1)}, u32[]{:S(2)}, u32[]{:S(2)}) collective-permute-start(bf16[2,64,2560]{2,1,0:T(8,128)(2,1)S(1)} %copy.49), channel_id=1, source_target_pairs={{64,0},{128,64},{192,128},{256,192},{320,256},{384,320},{448,384},... | collective-permute-start | bytes 1966088 | tf_op jit(solution)/shard_map/while/body/eval_jaxpr/ppermute | solution.py:142
  591.6 25.7 %all-to-all-start.1 = ((bf16[2,64,2560]{2,0,1:T(2,128)(2,1)}), bf16[2,64,2560]{2,0,1:T(2,128)(2,1)S(1)}, u32[]{:S(2)}, u32[]{:S(2)}) async-start(bf16[2,64,2560]{2,0,1:T(2,128)(2,1)} %copy.48), calls=%async_computation.1 | async-start | bytes 1310720 | tf_op jit(solution)/shard_map/while/body/eval_jaxpr/all_to_all | solution.py:139
  617.4 20.4 %collective-permute-start.1 = (bf16[2,64,2560]{2,1,0:T(8,128)(2,1)S(1)}, bf16[2,64,2560]{2,1,0:T(8,128)(2,1)S(1)}, u32[]{:S(2)}, u32[]{:S(2)}) collective-permute-start(bf16[2,64,2560]{2,1,0:T(8,128)(2,1)S(1)} %copy.49), channel_id=1, source_target_pairs={{64,0},{128,64},{192,128},{256,192},{320,256},{384,320},{448,384},... | collective-permute-start | bytes 1966088 | tf_op jit(solution)/shard_map/while/body/eval_jaxpr/ppermute | solution.py:142
  643.1 25.7 %all-to-all-start.1 = ((bf16[2,64,2560]{2,0,1:T(2,128)(2,1)}), bf16[2,64,2560]{2,0,1:T(2,128)(2,1)S(1)}, u32[]{:S(2)}, u32[]{:S(2)}) async-start(bf16[2,64,2560]{2,0,1:T(2,128)(2,1)} %copy.48), calls=%async_computation.1 | async-start | bytes 1310720 | tf_op jit(solution)/shard_map/while/body/eval_jaxpr/all_to_all | solution.py:139
  668.8 20.5 %collective-permute-start.1 = (bf16[2,64,2560]{2,1,0:T(8,128)(2,1)S(1)}, bf16[2,64,2560]{2,1,0:T(8,128)(2,1)S(1)}, u32[]{:S(2)}, u32[]{:S(2)}) collective-permute-start(bf16[2,64,2560]{2,1,0:T(8,128)(2,1)S(1)} %copy.49), channel_id=1, source_target_pairs={{64,0},{128,64},{192,128},{256,192},{320,256},{384,320},{448,384},... | collective-permute-start | bytes 1966088 | tf_op jit(solution)/shard_map/while/body/eval_jaxpr/ppermute | solution.py:142
  694.6 25.7 %all-to-all-start.1 = ((bf16[2,64,2560]{2,0,1:T(2,128)(2,1)}), bf16[2,64,2560]{2,0,1:T(2,128)(2,1)S(1)}, u32[]{:S(2)}, u32[]{:S(2)}) async-start(bf16[2,64,2560]{2,0,1:T(2,128)(2,1)} %copy.48), calls=%async_computation.1 | async-start | bytes 1310720 | tf_op jit(solution)/shard_map/while/body/eval_jaxpr/all_to_all | solution.py:139
  720.3 20.5 %collective-permute-start.1 = (bf16[2,64,2560]{2,1,0:T(8,128)(2,1)S(1)}, bf16[2,64,2560]{2,1,0:T(8,128)(2,1)S(1)}, u32[]{:S(2)}, u32[]{:S(2)}) collective-permute-start(bf16[2,64,2560]{2,1,0:T(8,128)(2,1)S(1)} %copy.49), channel_id=1, source_target_pairs={{64,0},{128,64},{192,128},{256,192},{320,256},{384,320},{448,384},... | collective-permute-start | bytes 1966088 | tf_op jit(solution)/shard_map/while/body/eval_jaxpr/ppermute | solution.py:142
  (113 other events, 916.5 us)

commit v7 on v4

--- a/solution.py
+++ b/solution.py
@@ -67,10 +67,6 @@
 
     x = inputs.reshape(micro_count, batch_rows, feature_count)
     keep_x = jnp.zeros((row_count, feature_count), jnp.bfloat16)
-    keep_inv = jnp.zeros((row_count, 1), jnp.float32)
-    keep_normed = jnp.zeros((row_count, feature_count), jnp.bfloat16)
-    keep_active = jnp.zeros((row_count, down_proj.shape[0]), jnp.bfloat16)
-    keep_slope = jnp.zeros((row_count, down_proj.shape[0]), jnp.float32)
     upstream = None
     for k in range(sections):
         flat = x.reshape(row_count, feature_count)
@@ -81,12 +77,7 @@
         outputs = (x_float + jnp.dot(active, up_proj, preferred_element_type=jnp.float32)).astype(
             jnp.bfloat16
         )
-        mine = section_now == k
-        keep_x = jnp.where(mine, flat, keep_x)
-        keep_inv = jnp.where(mine, inv_rms, keep_inv)
-        keep_normed = jnp.where(mine, normed, keep_normed)
-        keep_active = jnp.where(mine, active, keep_active)
-        keep_slope = jnp.where(mine, gelu_slope, keep_slope)
+        keep_x = jnp.where(section_now == k, flat, keep_x)
         if k < sections - 1:
             packed = permute_rows(
                 send_onehot[k], outputs.reshape(micro_count, batch_rows, feature_count), "mdq,mqf->mdf"
@@ -96,7 +87,9 @@
         else:
             upstream = outputs
 
-    x_float = keep_x.astype(jnp.float32)
+    x_float, keep_inv, keep_normed = normalize(keep_x, gain_row)
+    gelu_value, keep_slope = gelu_parts(contract_last(keep_normed, down_proj))
+    keep_active = gelu_value.astype(jnp.bfloat16)
     keep_upstream = jnp.zeros((row_count, feature_count), jnp.bfloat16)
     keep_grad_hidden = jnp.zeros((row_count, down_proj.shape[0]), jnp.bfloat16)
     for k in reversed(range(sections)):

time: 752 us -> 774 us (1.029)
  matrix products: 29.1 us -> 48.4 us
    dot_general x8, matrix products: 4.26 us -> 23 us  [local(): jnp.dot(active, up_proj, preferred_element_type=jnp.float32)]
  transfers between devices with their start and end apart: 21 -> 21, of which waited for: 9 -> 9; matrix products, arithmetic and copies ran while one was open for 1% -> 0% of each run, Pallas kernels for 0% -> 0%
where the time goes in v7:
time: 774 us; the launch traced here: 765 us
  blocking collectives  346 us (45%)
  waiting for transfers between devices  281 us (36%)
  matrix products  48.4 us (6%)
  starting transfers between devices  38.1 us (5%)
  other arithmetic  25.5 us (3%)
  local copies, waits for them, and re-layouts  23.6 us (3%)
    ppermute x7, waiting for transfers between devices, local(): moved = lax.ppermute(sent, 'section', [(k, k - 1)])  213 us
    all_to_all x7, blocking collectives, local(): received = lax.all_to_all(packed, 'peer', 1, 1, tiled=True)  189 us
    all_to_all x6, blocking collectives, local(): lax.all_to_all(grad_rows.reshape(micro_count, batch_rows, feature_count),...  157 us
    ppermute x6, waiting for transfers between devices, local(): arrived = lax.ppermute(outgoing.astype(jnp.bfloat16), 'peer', pairs)  33.8 us
    dot_general x8, matrix products, local(): jnp.dot(active, up_proj, preferred_element_type=jnp.float32)  23 us
    all_to_all x1, waiting for transfers between devices, local(): lax.all_to_all(grad_rows.reshape(micro_count, batch_rows, feature_count),...  19.1 us
    dot_general x14, matrix products, permute_rows(): jnp.einsum(spec, onehot, rows, preferred_element_type=jnp.float32)  16.7 us
    ppermute x6, starting transfers between devices, local(): arrived = lax.ppermute(outgoing.astype(jnp.bfloat16), 'peer', pairs)  16 us
  transfers between devices with their start and end apart: 21, of which 9 were waited for; matrix products, arithmetic and copies ran while one was open for 0% of the time, Pallas kernels for 0%

profile of v7, /device:TPU:6, one launch (start us, length us, event | category | flops | bytes accessed | tf_op | source)
XLA Modules:
  0.0 764.7 jit_solution(16716248409956532534)
XLA Ops:
  8.6 33.1 %all_to_all.70 = bf16[2,64,2560]{2,0,1:T(2,128)(2,1)S(1)} all-to-all(bf16[2,64,2560]{2,0,1:T(2,128)(2,1)S(1)} %copy.104), channel_id=1, replica_groups=mesh['section'=8,'peer'=64] {'peer'}, dimensions={1} | all-to-all | bytes 1310720 | tf_op jit(solution)/shard_map/all_to_all | solution.py:85
  41.8 3.7 collective-permute-start
  45.5 14.9 %collective-permute-done = bf16[2,64,2560]{2,1,0:T(8,128)(2,1)S(1)} collective-permute-done((bf16[2,64,2560]{2,1,0:T(8,128)(2,1)S(1)}, bf16[2,64,2560]{2,1,0:T(8,128)(2,1)S(1)}, u32[]{:S(2)}, u32[]{:S(2)}) %collective-permute-start) | collective-permute-done | bytes 655392 | tf_op jit(solution)/shard_map/ppermute | solution.py:86
  64.8 25.2 %all_to_all.71 = bf16[2,64,2560]{2,0,1:T(2,128)(2,1)S(1)} all-to-all(bf16[2,64,2560]{2,0,1:T(2,128)(2,1)S(1)} %copy.106), channel_id=1, replica_groups=mesh['section'=8,'peer'=64] {'peer'}, dimensions={1} | all-to-all | bytes 1310720 | tf_op jit(solution)/shard_map/all_to_all | solution.py:85
  97.3 26.2 %all_to_all.72 = bf16[2,64,2560]{2,0,1:T(2,128)(2,1)S(1)} all-to-all(bf16[2,64,2560]{2,0,1:T(2,128)(2,1)S(1)} %copy.108), channel_id=1, replica_groups=mesh['section'=8,'peer'=64] {'peer'}, dimensions={1} | all-to-all | bytes 1310720 | tf_op jit(solution)/shard_map/all_to_all | solution.py:85
  131.2 26.2 %all_to_all.73 = bf16[2,64,2560]{2,0,1:T(2,128)(2,1)S(1)} all-to-all(bf16[2,64,2560]{2,0,1:T(2,128)(2,1)S(1)} %copy.110), channel_id=1, replica_groups=mesh['section'=8,'peer'=64] {'peer'}, dimensions={1} | all-to-all | bytes 1310720 | tf_op jit(solution)/shard_map/all_to_all | solution.py:85
  164.5 26.2 %all_to_all.74 = bf16[2,64,2560]{2,0,1:T(2,128)(2,1)S(1)} all-to-all(bf16[2,64,2560]{2,0,1:T(2,128)(2,1)S(1)} %copy.112), channel_id=1, replica_groups=mesh['section'=8,'peer'=64] {'peer'}, dimensions={1} | all-to-all | bytes 1310720 | tf_op jit(solution)/shard_map/all_to_all | solution.py:85
  197.9 26.2 %all_to_all.75 = bf16[2,64,2560]{2,0,1:T(2,128)(2,1)S(1)} all-to-all(bf16[2,64,2560]{2,0,1:T(2,128)(2,1)S(1)} %copy.114), channel_id=1, replica_groups=mesh['section'=8,'peer'=64] {'peer'}, dimensions={1} | all-to-all | bytes 1310720 | tf_op jit(solution)/shard_map/all_to_all | solution.py:85
  231.2 26.3 %all_to_all.76 = bf16[2,64,2560]{2,0,1:T(2,128)(2,1)S(1)} all-to-all(bf16[2,64,2560]{2,0,1:T(2,128)(2,1)S(1)} %copy.116), channel_id=1, replica_groups=mesh['section'=8,'peer'=64] {'peer'}, dimensions={1} | all-to-all | bytes 1310720 | tf_op jit(solution)/shard_map/all_to_all | solution.py:85
  266.4 3.2 add_convert_fusion
  273.4 26.2 %all_to_all.77 = bf16[2,64,2560]{2,0,1:T(2,128)(2,1)S(1)} all-to-all(bf16[2,64,2560]{2,0,1:T(2,128)(2,1)S(1)} %copy.118), channel_id=1, replica_groups=mesh['section'=8,'peer'=64] {'peer'}, dimensions={1} | all-to-all | bytes 1310720 | tf_op jit(solution)/shard_map/all_to_all | solution.py:108
  303.5 26.2 %all_to_all.78 = bf16[2,64,2560]{2,0,1:T(2,128)(2,1)S(1)} all-to-all(bf16[2,64,2560]{2,0,1:T(2,128)(2,1)S(1)} %copy.121), channel_id=1, replica_groups=mesh['section'=8,'peer'=64] {'peer'}, dimensions={1} | all-to-all | bytes 1310720 | tf_op jit(solution)/shard_map/all_to_all | solution.py:108
  333.7 26.2 %all_to_all.79 = bf16[2,64,2560]{2,0,1:T(2,128)(2,1)S(1)} all-to-all(bf16[2,64,2560]{2,0,1:T(2,128)(2,1)S(1)} %copy.124), channel_id=1, replica_groups=mesh['section'=8,'peer'=64] {'peer'}, dimensions={1} | all-to-all | bytes 1310720 | tf_op jit(solution)/shard_map/all_to_all | solution.py:108
  364.0 26.2 %all_to_all.80 = bf16[2,64,2560]{2,0,1:T(2,128)(2,1)S(1)} all-to-all(bf16[2,64,2560]{2,0,1:T(2,128)(2,1)S(1)} %copy.127), channel_id=1, replica_groups=mesh['section'=8,'peer'=64] {'peer'}, dimensions={1} | all-to-all | bytes 1310720 | tf_op jit(solution)/shard_map/all_to_all | solution.py:108
  394.2 26.2 %all_to_all.81 = bf16[2,64,2560]{2,0,1:T(2,128)(2,1)S(1)} all-to-all(bf16[2,64,2560]{2,0,1:T(2,128)(2,1)S(1)} %copy.130), channel_id=1, replica_groups=mesh['section'=8,'peer'=64] {'peer'}, dimensions={1} | all-to-all | bytes 1310720 | tf_op jit(solution)/shard_map/all_to_all | solution.py:108
  424.5 26.2 %all_to_all.82 = bf16[2,64,2560]{2,0,1:T(2,128)(2,1)S(1)} all-to-all(bf16[2,64,2560]{2,0,1:T(2,128)(2,1)S(1)} %copy.133), channel_id=1, replica_groups=mesh['section'=8,'peer'=64] {'peer'}, dimensions={1} | all-to-all | bytes 1310720 | tf_op jit(solution)/shard_map/all_to_all | solution.py:108
  455.9 7.2 all-to-all-start.13
  463.2 19.1 %all-to-all-done.13 = bf16[2,64,2560]{2,0,1:T(2,128)(2,1)} async-done(((bf16[2,64,2560]{2,0,1:T(2,128)(2,1)}), bf16[2,64,2560]{2,0,1:T(2,128)(2,1)}, u32[]{:S(2)}, u32[]{:S(2)}) %all-to-all-start.13) | async-done | bytes 655392 | tf_op jit(solution)/shard_map/all_to_all | solution.py:108
  486.1 213.4 %collective-permute-done.13 = bf16[2,64,2560]{2,1,0:T(8,128)(2,1)} collective-permute-done((bf16[2,64,2560]{2,1,0:T(8,128)(2,1)}, bf16[2,64,2560]{2,1,0:T(8,128)(2,1)}, u32[]{:S(2)}, u32[]{:S(2)}) %collective-permute-start.13) | collective-permute-done | bytes 655392 | tf_op jit(solution)/shard_map/ppermute | solution.py:111
  719.3 8.0 %collective-permute-done.15 = bf16[96,2560]{1,0:T(8,128)(2,1)S(1)} collective-permute-done((bf16[96,2560]{1,0:T(8,128)(2,1)S(1)}, bf16[96,2560]{1,0:T(8,128)(2,1)S(1)}, u32[]{:S(2)}, u32[]{:S(2)}) %collective-permute-start.15) | collective-permute-done | bytes 491552 | tf_op jit(solution)/shard_map/ppermute | solution.py:150
  731.3 5.4 collective-permute-done.16
  739.3 6.5 collective-permute-done.17
  749.1 4.7 collective-permute-done.18
  756.8 6.7 collective-permute-done.19
  (241 shorter events, 123.9 us)
Async XLA Ops:
  2.8 226.4 %copy-start.20 = (pred[7,2,64,64]{3,2,1,0:T(32,128)(4,1)}, pred[7,2,64,64]{3,2,1,0:T(32,128)(4,1)S(1)}, u32[]{:S(2)}) copy-start(pred[7,2,64,64]{3,2,1,0:T(32,128)(4,1)S(1)} %iota_compare_fusion) | copy-start | bytes 172036
  41.8 18.6 %collective-permute-start = (bf16[2,64,2560]{2,1,0:T(8,128)(2,1)S(1)}, bf16[2,64,2560]{2,1,0:T(8,128)(2,1)S(1)}, u32[]{:S(2)}, u32[]{:S(2)}) collective-permute-start(bf16[2,64,2560]{2,1,0:T(8,128)(2,1)S(1)} %copy.105), channel_id=1, source_target_pairs={{0,64},{1,65},{2,66},{3,67},{4,68},{5,69},{6,70},{7,71},{8,72},{9,... | collective-permute-start | bytes 1966088 | tf_op jit(solution)/shard_map/ppermute | solution.py:86
  90.2 0.7 collective-permute-start.1
  123.5 1.2 collective-permute-start.2
  157.4 0.7 collective-permute-start.3
  190.8 0.7 collective-permute-start.4
  224.1 0.7 collective-permute-start.5
  257.6 1.5 collective-permute-start.6
  299.6 0.7 collective-permute-start.7
  329.7 0.7 collective-permute-start.8
  360.0 0.7 collective-permute-start.9
  390.2 0.7 collective-permute-start.10
  420.5 0.7 collective-permute-start.11
  450.7 1.0 collective-permute-start.12
  455.9 26.5 %all-to-all-start.13 = ((bf16[2,64,2560]{2,0,1:T(2,128)(2,1)}), bf16[2,64,2560]{2,0,1:T(2,128)(2,1)}, u32[]{:S(2)}, u32[]{:S(2)}) async-start(bf16[2,64,2560]{2,0,1:T(2,128)(2,1)} %copy.136), calls=%async_computation.13 | async-start | bytes 1310720 | tf_op jit(solution)/shard_map/all_to_all | solution.py:108
  463.2 237.8 %copy-start.10 = (bf16[2,64,2560]{2,1,0:T(8,128)(2,1)S(1)}, bf16[2,64,2560]{2,1,0:T(8,128)(2,1)}, u32[]{:S(2)}) copy-start(bf16[2,64,2560]{2,1,0:T(8,128)(2,1)} %copy-done.9) | copy-start | bytes 1966084
  484.4 215.1 %collective-permute-start.13 = (bf16[2,64,2560]{2,1,0:T(8,128)(2,1)}, bf16[2,64,2560]{2,1,0:T(8,128)(2,1)}, u32[]{:S(2)}, u32[]{:S(2)}) collective-permute-start(bf16[2,64,2560]{2,1,0:T(8,128)(2,1)} %copy.137), channel_id=1, source_target_pairs={{64,0},{65,1},{66,2},{67,3},{68,4},{69,5},{70,6},{71,7},{72,8},{73... | collective-permute-start | bytes 1966088 | tf_op jit(solution)/shard_map/ppermute | solution.py:111
  486.0 215.0 %copy-start.12 = (bf16[2,64,2560]{2,1,0:T(8,128)(2,1)S(1)}, bf16[2,64,2560]{2,1,0:T(8,128)(2,1)}, u32[]{:S(2)}) copy-start(bf16[2,64,2560]{2,1,0:T(8,128)(2,1)} %copy-done.11) | copy-start | bytes 1966084
  709.0 4.5 collective-permute-start.14
  716.6 10.7 %collective-permute-start.15 = (bf16[96,2560]{1,0:T(8,128)(2,1)S(1)}, bf16[96,2560]{1,0:T(8,128)(2,1)S(1)}, u32[]{:S(2)}, u32[]{:S(2)}) collective-permute-start(bf16[96,2560]{1,0:T(8,128)(2,1)S(1)} %dynamic-slice_convert_fusion.1), channel_id=1, source_target_pairs={{0,2},{1,17},{2,0},{3,19},{4,6},{5,21},{6,4},{7,23},{8,10},{9,25},... | collective-permute-start | bytes 1474568 | tf_op jit(solution)/shard_map/ppermute | solution.py:150
  728.6 8.1 %collective-permute-start.16 = (bf16[48,2560]{1,0:T(8,128)(2,1)S(1)}, bf16[48,2560]{1,0:T(8,128)(2,1)S(1)}, u32[]{:S(2)}, u32[]{:S(2)}) collective-permute-start(bf16[48,2560]{1,0:T(8,128)(2,1)S(1)} %dynamic-slice_convert_fusion.2), channel_id=1, source_target_pairs={{0,16},{1,3},{2,18},{3,1},{4,20},{5,7},{6,22},{7,5},{8,24},{9,11},... | collective-permute-start | bytes 737288 | tf_op jit(solution)/shard_map/ppermute | solution.py:150
  736.8 9.0 %collective-permute-start.17 = (bf16[24,2560]{1,0:T(8,128)(2,1)S(1)}, bf16[24,2560]{1,0:T(8,128)(2,1)S(1)}, u32[]{:S(2)}, u32[]{:S(2)}) collective-permute-start(bf16[24,2560]{1,0:T(8,128)(2,1)S(1)} %dynamic-slice_convert_fusion.3), channel_id=1, source_target_pairs={{0,4},{1,33},{2,6},{3,35},{4,0},{5,37},{6,2},{7,39},{8,12},{9,41},... | collective-permute-start | bytes 368648 | tf_op jit(solution)/shard_map/ppermute | solution.py:150
  745.9 7.8 %collective-permute-start.18 = (bf16[12,2560]{1,0:T(8,128)(2,1)S(1)}, bf16[12,2560]{1,0:T(8,128)(2,1)S(1)}, u32[]{:S(2)}, u32[]{:S(2)}) collective-permute-start(bf16[12,2560]{1,0:T(8,128)(2,1)S(1)} %dynamic-slice_convert_fusion.4), channel_id=1, source_target_pairs={{0,32},{1,5},{2,34},{3,7},{4,36},{5,1},{6,38},{7,3},{8,40},{9,13},... | collective-permute-start | bytes 184328 | tf_op jit(solution)/shard_map/ppermute | solution.py:150
  753.8 9.8 %collective-permute-start.19 = (bf16[6,2560]{1,0:T(8,128)(2,1)S(1)}, bf16[6,2560]{1,0:T(8,128)(2,1)S(1)}, u32[]{:S(2)}, u32[]{:S(2)}) collective-permute-start(bf16[6,2560]{1,0:T(8,128)(2,1)S(1)} %dynamic-slice_convert_fusion.5), channel_id=1, source_target_pairs={{0,8},{1,9},{2,10},{3,11},{4,12},{5,13},{6,14},{7,15},{8,0},{9,1},... | collective-permute-start | bytes 92168 | tf_op jit(solution)/shard_map/ppermute | solution.py:150
  (29 other events, 298.2 us)
